TPU v7x, 256 devices: a whole 4x4x8 slice. The times are simulated.
256 devices in a mesh: grp: 32 (over y, x, core), dev: 8 (over z).
Axes of the slice: x: 4, y: 4, z: 8, core: 2. Of those that a mesh axis runs over, the one named last changes fastest.
Arguments:
- rows: bfloat16 [524288, 1024], P(('grp', 'dev')), may hold values from -24 to 24
- lengths: int32 [32, 8], P('grp', 'dev'), may hold values from 1 to 2048, 8192 in all within a row
- sketch_block: int32 [524288], P(('grp', 'dev')), may hold values from 0 to 511
- sketch_sign: int32 [524288], P(('grp', 'dev')), may hold values from 0 to 1
Outputs:
- scores: float32 [524288], P(('grp', 'dev'))
Inputs may be any that keep to these rules, and one draw needn't show every extreme that they name: The lengths of the 8 devices of one index of grp sum to 8192; the largest is 2048 in every such group.
All inputs are finite; a program needn't handle non-finite values.
Results may differ from a plain program's by a relative error of at most 0.00084.
Values may be sent and summed in bfloat16 or wider, within the bound.
No kernel may reach another device: no remote copies, remote signals or barrier semaphores. Data moves between devices by JAX's collectives and lax.ppermute only.
A program may use at most 128 MiB of HBM per device.

v0:
```python
import jax
import jax.numpy as jnp
from jax import lax
from jax.sharding import PartitionSpec as P

MEAN = 1024
SK_DEV = 512


def add_gram(row_piece):
    return lax.dot_general(
        row_piece, row_piece, (((0,), (0,)), ((), ())), preferred_element_type=jnp.float32
    )


def shards(rows, lengths, sketch_block, sketch_sign):
    capacity = rows.shape[0]
    features = rows.shape[1]
    row_count = lengths.reshape(())
    slot_index = lax.iota(jnp.int32, capacity)
    is_live = slot_index < row_count
    row_sign = jnp.where(is_live, 2 * sketch_sign - 1, 0).astype(jnp.bfloat16)
    picker = (lax.iota(jnp.int32, SK_DEV)[:, None] == sketch_block[None, :]).astype(
        jnp.bfloat16
    ) * row_sign[None, :]
    sketched = jnp.dot(picker, rows, preferred_element_type=jnp.float32).astype(jnp.bfloat16)
    gram_matrix = lax.psum(add_gram(sketched), ("grp", "dev"))
    ridge_value = float(lax.axis_size("grp") * lax.axis_size("dev") * MEAN)
    identity_matrix = jnp.eye(features, dtype=jnp.float32)
    lower_factor = jnp.linalg.cholesky(gram_matrix + ridge_value * identity_matrix)
    inverse = lax.linalg.triangular_solve(lower_factor, identity_matrix, left_side=True, lower=True)
    weight = inverse.T.astype(jnp.bfloat16)
    factor = ridge_value / features
    projected = jnp.dot(rows, weight, preferred_element_type=jnp.float32)
    return jnp.where(is_live, factor * jnp.sum(projected * projected, axis=1), 0.0)


def solution(mesh):
    in_specs = (P(("grp", "dev"), None), P("grp", "dev"), P(("grp", "dev")), P(("grp", "dev")))
    out_specs = P(("grp", "dev"))
    return jax.shard_map(shards, mesh=mesh, in_specs=in_specs, out_specs=out_specs, check_vma=False)
```

profile of v0, /device:TPU:2, one launch (start us, length us, event | category | flops | bytes accessed | tf_op | source)
XLA Modules:
  0.0 674.6 jit_solution(6037391347249158607)
XLA Ops:
  7.9 11.1 %fusion.36 = f32[1024,1024]{0,1:T(8,128)} fusion(bf16[2048,1024]{1,0:T(8,128)(2,1)} %param.4, s32[2048]{0:T(1024)} %param.6, bf16[2048]{0:T(1024)(128)(2,1)S(1)} %select_convert_fusion), kind=kOutput, calls=%fused_computation.56 | convolution fusion | flops 3223846912 | bytes 8400896 | tf_op jit(solution)/shard_map/dot_general | solution.py:11
  19.3 2.4 fusion.2
  21.7 270.5 %all-reduce.3.cloned.1.call-done = f32[1024,1024]{0,1:T(8,128)} async-done(((f32[1024,1024]{0,1:T(8,128)}), f32[1024,1024]{0,1:T(8,128)}) %all-reduce.3.cloned.1.call-update) | async-done | bytes 4194320 | tf_op jit(solution)/shard_map/psum | solution.py:27
  292.3 4.8 select_add_fusion
  297.1 5.5 copy.6
  302.6 4.5 fusion
  307.0 2.0 copy-done.2
  309.0 11.7 %cholesky.222 = f32[128,128]{1,0:T(8,128)S(1)} custom-call(f32[128,128]{1,0:T(8,128)S(1)} %cholesky.577), custom_call_target="Cholesky" | custom-call | tf_op jit(solution)/shard_map/jit(cholesky)/cholesky | solution.py:30
  320.9 9.8 %custom-call.62 = f32[1,128,128]{1,2,0:T(8,128)S(1)} custom-call(f32[1,128,128]{2,1,0:T(8,128)S(1)} %get-tuple-element.57), custom_call_target="InvertDiagBlocksLowerTriangular" | custom-call | tf_op jit(solution)/shard_map/jit(cholesky)/cholesky | solution.py:30
  334.0 11.7 %cholesky.243 = f32[128,128]{1,0:T(8,128)S(1)} custom-call(f32[128,128]{1,0:T(8,128)S(1)} %cholesky.581), custom_call_target="Cholesky" | custom-call | tf_op jit(solution)/shard_map/jit(cholesky)/cholesky | solution.py:30
  346.1 9.8 %custom-call.63 = f32[1,128,128]{1,2,0:T(8,128)S(1)} custom-call(f32[1,128,128]{2,1,0:T(8,128)S(1)} %get-tuple-element.55), custom_call_target="InvertDiagBlocksLowerTriangular" | custom-call | tf_op jit(solution)/shard_map/jit(cholesky)/cholesky | solution.py:30
  357.0 2.0 copy-done
  359.0 2.4 convolution_subtract_fusion.6
  361.4 11.7 %cholesky.466 = f32[128,128]{1,0:T(8,128)S(1)} custom-call(f32[128,128]{1,0:T(8,128)S(1)} %cholesky.586), custom_call_target="Cholesky" | custom-call | tf_op jit(solution)/shard_map/jit(cholesky)/cholesky | solution.py:30
  373.9 9.8 %custom-call.64 = f32[1,128,128]{1,2,0:T(8,128)S(1)} custom-call(f32[1,128,128]{2,1,0:T(8,128)S(1)} %get-tuple-element.53), custom_call_target="InvertDiagBlocksLowerTriangular" | custom-call | tf_op jit(solution)/shard_map/jit(cholesky)/cholesky | solution.py:30
  384.9 3.5 convolution_subtract_fusion.7
  388.4 11.7 %cholesky.485 = f32[128,128]{1,0:T(8,128)S(1)} custom-call(f32[128,128]{1,0:T(8,128)S(1)} %cholesky.591), custom_call_target="Cholesky" | custom-call | tf_op jit(solution)/shard_map/jit(cholesky)/cholesky | solution.py:30
  400.9 9.8 %custom-call.65 = f32[1,128,128]{1,2,0:T(8,128)S(1)} custom-call(f32[1,128,128]{2,1,0:T(8,128)S(1)} %get-tuple-element.51), custom_call_target="InvertDiagBlocksLowerTriangular" | custom-call | tf_op jit(solution)/shard_map/jit(cholesky)/cholesky | solution.py:30
  411.9 3.2 convolution_subtract_fusion.8
  415.0 11.9 %cholesky.504 = f32[128,128]{1,0:T(8,128)S(1)} custom-call(f32[128,128]{1,0:T(8,128)S(1)} %cholesky.596), custom_call_target="Cholesky" | custom-call | tf_op jit(solution)/shard_map/jit(cholesky)/cholesky | solution.py:30
  427.7 9.8 %custom-call.66 = f32[1,128,128]{1,2,0:T(8,128)S(1)} custom-call(f32[1,128,128]{2,1,0:T(8,128)S(1)} %get-tuple-element.49), custom_call_target="InvertDiagBlocksLowerTriangular" | custom-call | tf_op jit(solution)/shard_map/jit(cholesky)/cholesky | solution.py:30
  438.6 3.2 convolution_subtract_fusion.9
  441.9 11.7 %cholesky.524 = f32[128,128]{1,0:T(8,128)S(1)} custom-call(f32[128,128]{1,0:T(8,128)S(1)} %cholesky.601), custom_call_target="Cholesky" | custom-call | tf_op jit(solution)/shard_map/jit(cholesky)/cholesky | solution.py:30
  454.4 9.8 %custom-call.67 = f32[1,128,128]{1,2,0:T(8,128)S(1)} custom-call(f32[1,128,128]{2,1,0:T(8,128)S(1)} %get-tuple-element.47), custom_call_target="InvertDiagBlocksLowerTriangular" | custom-call | tf_op jit(solution)/shard_map/jit(cholesky)/cholesky | solution.py:30
  465.2 3.1 convolution_subtract_fusion.10
  468.4 11.7 %cholesky.544 = f32[128,128]{1,0:T(8,128)S(1)} custom-call(f32[128,128]{1,0:T(8,128)S(1)} %cholesky.606), custom_call_target="Cholesky" | custom-call | tf_op jit(solution)/shard_map/jit(cholesky)/cholesky | solution.py:30
  480.8 9.8 %custom-call.68 = f32[1,128,128]{1,2,0:T(8,128)S(1)} custom-call(f32[1,128,128]{2,1,0:T(8,128)S(1)} %get-tuple-element.45), custom_call_target="InvertDiagBlocksLowerTriangular" | custom-call | tf_op jit(solution)/shard_map/jit(cholesky)/cholesky | solution.py:30
  491.6 2.2 convolution_subtract_fusion.11
  493.8 11.7 %cholesky.562 = f32[128,128]{1,0:T(8,128)S(1)} custom-call(f32[128,128]{1,0:T(8,128)S(1)} %convolution_subtract_fusion.11), custom_call_target="Cholesky" | custom-call | tf_op jit(solution)/shard_map/jit(cholesky)/cholesky | solution.py:30
  515.9 4.9 select_select_fusion
  520.7 23.4 %while.1 = (s32[]{:T(128)}, f32[1024,1024]{0,1:T(8,128)}, s32[8,2]{0,1:T(2,128)S(1)}, f32[8,128,128]{2,1,0:T(8,128)S(1)}, s32[]{:T(128)}) while((s32[]{:T(128)}, f32[1024,1024]{0,1:T(8,128)}, s32[8,2]{0,1:T(2,128)S(1)}, f32[8,128,128]{2,1,0:T(8,128)S(1)}, s32[]{:T(128)}) %tuple.46), condition=%wide.while_cond, body=%wide.while_body.sunk | while | flops 2 | bytes 393329 | solution.py:31
  521.3 2.2 dynamic-slice.7
  524.3 2.2 dynamic-slice.7
  527.2 2.2 dynamic-slice.7
  530.1 2.2 dynamic-slice.7
  533.1 2.2 dynamic-slice.7
  536.0 2.2 dynamic-slice.7
  538.9 2.2 dynamic-slice.7
  541.9 2.1 dynamic-slice.7
  544.1 78.8 %custom-call.69 = f32[8,128,128]{1,2,0:T(8,128)S(1)} custom-call(f32[8,128,128]{2,1,0:T(8,128)S(1)} %get-tuple-element.12), custom_call_target="InvertDiagBlocksLowerTriangular" | custom-call | tf_op jit(solution)/shard_map/triangular_solve | solution.py:31
  623.5 2.4 convolution_subtract_fusion.4
  626.6 2.7 convolution_subtract_fusion
  630.0 3.7 fusion.23
  634.4 4.4 fusion.26
  640.4 5.4 convolution_subtract_fusion.2
  646.6 6.1 convolution_subtract_fusion.1
  653.5 7.8 %convolution_subtract_fusion.3 = f32[128,1024]{0,1:T(8,128)S(1)} fusion(f32[896,1024]{1,0:T(8,128)S(1)} %constant_dynamic-update-slice_fusion.11, f32[1024,1024]{0,1:T(8,128)S(1)} %copy-done.1, f32[1024,1024]{0,1:T(8,128)} %get-tuple-element.120), kind=kOutput, calls=%fused_computation.35 | convolution fusion | flops 1409417216 | bytes 5177344 | tf_op jit(solution)/shard_map/triangular_solve | solution.py:31
  661.9 4.8 multiply_reduce_fusion
  (109 shorter events, 33.1 us)
Async XLA Ops:
  6.5 285.7 %all-reduce.3.cloned.1.call-start = ((), (), s32[]{:S(2)}) async-start(), calls=%async_computation | async-start | bytes 8388608 | tf_op jit(solution)/shard_map/psum | solution.py:27
  307.0 2.0 copy-start.2
  357.0 2.0 copy-start
  622.9 3.7 copy-start.1
  652.8 9.2 %copy-start.3 = (bf16[2048,1024]{1,0:T(8,128)(2,1)S(1)}, bf16[2048,1024]{1,0:T(8,128)(2,1)}, u32[]{:S(2)}) copy-start(bf16[2048,1024]{1,0:T(8,128)(2,1)} %param.4) | copy-start | bytes 12582916
Sparse Core Ops, SparseCore 0:
  19.1 273.1 all-reduce.2
where the time goes:
time: 680 us; the launch traced here: 675 us
  waiting for transfers between devices  271 us (40%)
  other arithmetic  264 us (39%)
  matrix products  80.1 us (12%)
  local copies, waits for them, and re-layouts  39.4 us (6%)
  between operations  20 us (3%)
    psum x1, waiting for transfers between devices, shards(): gram_matrix = lax.psum(add_gram(sketched), ('grp', 'dev'))  271 us
    another operation x30, other arithmetic, shards(): jnp.linalg.cholesky(gram_matrix + ridge_value * identity_matrix)  167 us
    another operation x3, other arithmetic, shards(): lax.linalg.triangular_solve(lower_factor, identity_matrix, left_side=True...  83.6 us
    another operation x15, matrix products, shards(): lax.linalg.triangular_solve(lower_factor, identity_matrix, left_side=True...  37.6 us
    another operation x14, matrix products, shards(): jnp.linalg.cholesky(gram_matrix + ridge_value * identity_matrix)  26.6 us
    another operation x40, local copies, waits for them, and re-layouts  23.1 us
  transfers between devices with their start and end apart: 1, of which 1 were waited for; matrix products, arithmetic and copies ran while one was open for 0% of the time, Pallas kernels for 0%

commit v1 on v0

--- a/solution.py
+++ b/solution.py
@@ -5,12 +5,48 @@
 
 MEAN = 1024
 SK_DEV = 512
+BASE = 128
+HI = lax.Precision.HIGHEST
 
 
 def add_gram(row_piece):
     return lax.dot_general(
         row_piece, row_piece, (((0,), (0,)), ((), ())), preferred_element_type=jnp.float32
     )
+
+
+def mm(a, b):
+    return jnp.dot(a, b, precision=HI)
+
+
+def mmt(a, b):
+    return lax.dot_general(a, b, (((1,), (1,)), ((), ())), precision=HI)
+
+
+def chol_inv(a):
+    n = a.shape[0]
+    if n <= BASE:
+        lower = jnp.linalg.cholesky(a)
+        eye = jnp.eye(n, dtype=jnp.float32)
+        return lower, lax.linalg.triangular_solve(lower, eye, left_side=True, lower=True)
+    h = n // 2
+    l11, i11 = chol_inv(a[:h, :h])
+    l21 = mmt(a[h:, :h], i11)
+    l22, i22 = chol_inv(a[h:, h:] - mmt(l21, l21))
+    i21 = -mm(i22, mm(l21, i11))
+    z = jnp.zeros((h, n - h), jnp.float32)
+    return jnp.block([[l11, z], [l21, l22]]), jnp.block([[i11, z], [i21, i22]])
+
+
+def all_sum(g):
+    n_dev = lax.axis_size("dev")
+    n_grp = lax.axis_size("grp")
+    rows, cols = g.shape
+    part = lax.all_to_all(g.reshape(n_dev, rows // n_dev, cols), "dev", 0, 0, tiled=False).sum(0)
+    piece = rows // (n_dev * n_grp)
+    part = lax.all_to_all(part.reshape(n_grp, piece, cols), "grp", 0, 0, tiled=False).sum(0)
+    part = lax.all_gather(part, "grp", axis=0, tiled=True)
+    return lax.all_gather(part, "dev", axis=0, tiled=True)
 
 
 def shards(rows, lengths, sketch_block, sketch_sign):
@@ -24,11 +60,10 @@
         jnp.bfloat16
     ) * row_sign[None, :]
     sketched = jnp.dot(picker, rows, preferred_element_type=jnp.float32).astype(jnp.bfloat16)
-    gram_matrix = lax.psum(add_gram(sketched), ("grp", "dev"))
+    gram_matrix = all_sum(add_gram(sketched))
     ridge_value = float(lax.axis_size("grp") * lax.axis_size("dev") * MEAN)
     identity_matrix = jnp.eye(features, dtype=jnp.float32)
-    lower_factor = jnp.linalg.cholesky(gram_matrix + ridge_value * identity_matrix)
-    inverse = lax.linalg.triangular_solve(lower_factor, identity_matrix, left_side=True, lower=True)
+    _, inverse = chol_inv(gram_matrix + ridge_value * identity_matrix)
     weight = inverse.T.astype(jnp.bfloat16)
     factor = ridge_value / features
     projected = jnp.dot(rows, weight, preferred_element_type=jnp.float32)

time: 680 us -> 460 us (0.68)
  waiting for transfers between devices: 271 us -> 56.9 us
  blocking collectives: 0 us -> 146 us
  other arithmetic: 264 us -> 191 us
  matrix products: 80.1 us -> 40.9 us
  local copies, waits for them, and re-layouts: 39.4 us -> 4.36 us
    psum x1 -> x0, waiting for transfers between devices: 271 us -> none  [shards(): gram_matrix = lax.psum(add_gram(sketched), ('grp', 'dev'))]
    all_to_all x0 -> x2, blocking collectives: none -> 123 us  [the longest x1 105 us: all_sum(): lax.all_to_all(g.reshape(n_dev, rows // n_dev, cols), 'dev', 0, 0, tiled=...]
    another operation x33 -> x41, other arithmetic: 251 us -> 184 us  [the longest x24 99.9 us: chol_inv(): lower = jnp.linalg.cholesky(a)]
    another operation x29 -> x8, matrix products: 64.2 us -> 2.2 us  [chol_inv(): lax.linalg.triangular_solve(lower, eye, left_side=True, lower=True)]
    all_gather x0 -> x1, waiting for transfers between devices: none -> 56.9 us  [all_sum(): return lax.all_gather(part, 'dev', axis=0, tiled=True)]
    another operation x67 -> x4, local copies, waits for them, and re-layouts: 28.8 us -> 0.35 us  [chol_inv(): lax.linalg.triangular_solve(lower, eye, left_side=True, lower=True)]
    all_gather x0 -> x1, blocking collectives: none -> 23.4 us  [all_sum(): part = lax.all_gather(part, 'grp', axis=0, tiled=True)]
    dot_general x0 -> x28, matrix products: none -> 22.9 us  [the longest x14 15.6 us: mmt(): return lax.dot_general(a, b, (((1,), (1,)), ((), ())), precision=HI)]
where the time goes in v1:
time: 460 us; the launch traced here: 455 us
  other arithmetic  191 us (42%)
  blocking collectives  146 us (32%)
  waiting for transfers between devices  56.9 us (12%)
  matrix products  40.9 us (9%)
  between operations  15.1 us (3%)
    all_to_all x1, blocking collectives, all_sum(): lax.all_to_all(g.reshape(n_dev, rows // n_dev, cols), 'dev', 0, 0, tiled=...  105 us
    another operation x24, other arithmetic, chol_inv(): lower = jnp.linalg.cholesky(a)  99.9 us
    another operation x16, other arithmetic, chol_inv(): lax.linalg.triangular_solve(lower, eye, left_side=True, lower=True)  83.9 us
    all_gather x1, waiting for transfers between devices, all_sum(): return lax.all_gather(part, 'dev', axis=0, tiled=True)  56.9 us
    all_gather x1, blocking collectives, all_sum(): part = lax.all_gather(part, 'grp', axis=0, tiled=True)  23.4 us
    all_to_all x1, blocking collectives, all_sum(): lax.all_to_all(part.reshape(n_grp, piece, cols), 'grp', 0, 0, tiled=False)  17.8 us
    dot_general x14, matrix products, mmt(): return lax.dot_general(a, b, (((1,), (1,)), ((), ())), precision=HI)  15.6 us
    dot_general x1, matrix products, add_gram(): lax.dot_general(row_piece, row_piece, (((0,), (0,)), ((), ())), preferred...  11 us
  transfers between devices with their start and end apart: 1, of which 1 were waited for; matrix products, arithmetic and copies ran while one was open for 0% of the time, Pallas kernels for 0%

profile of v1, /device:TPU:2, one launch (start us, length us, event | category | flops | bytes accessed | tf_op | source)
XLA Modules:
  0.0 454.6 jit_solution(2378060399549380852)
XLA Ops:
  7.2 0.7 select_convert_fusion
  7.9 11.0 %fusion.21 = f32[1024,1024]{1,0:T(8,128)} fusion(bf16[2048,1024]{1,0:T(8,128)(2,1)} %param.7, s32[2048]{0:T(1024)} %param.9, bf16[2048]{0:T(1024)(128)(2,1)S(1)} %select_convert_fusion), kind=kOutput, calls=%fused_computation.38 | convolution fusion | flops 3223846912 | bytes 8400896 | tf_op jit(solution)/shard_map/dot_general | solution.py:13
  18.9 104.7 %all_to_all.10 = f32[8,128,1024]{2,1,0:T(8,128)} all-to-all(f32[8,128,1024]{2,1,0:T(8,128)} %bitcast.119), channel_id=1, replica_groups=mesh['grp'=32,'dev'=8] {'dev'}, dimensions={0} | all-to-all | bytes 8388608 | tf_op jit(solution)/shard_map/all_to_all | solution.py:45
  123.6 2.6 reduce_sum.27
  126.4 17.8 %all_to_all.11 = f32[32,4,1024]{2,1,0:T(4,128)S(1)} all-to-all(f32[32,4,1024]{2,1,0:T(4,128)S(1)} %reshape.24), channel_id=1, replica_groups=mesh['grp'=32,'dev'=8] {'grp'}, dimensions={0} | all-to-all | bytes 1048576 | tf_op jit(solution)/shard_map/all_to_all | solution.py:47
  144.3 23.4 %all-gather = f32[32,4,1024]{2,1,0:T(4,128)S(1)} all-gather(f32[1,4,1024]{2,1,0:T(4,128)S(1)} %bitcast.120), channel_id=1, replica_groups=mesh['grp'=32,'dev'=8] {'grp'}, dimensions={0}, use_global_device_ids=true | all-gather | bytes 540672 | tf_op jit(solution)/shard_map/all_gather | solution.py:48
  167.8 1.0 copy.111
  168.8 56.9 %all-gather.3.cloned.1.call-done = f32[1024,1024]{0,1:T(8,128)} async-done(((f32[128,1024]{0,1:T(8,128)}), f32[1024,1024]{0,1:T(8,128)}) %all-gather.3.cloned.1.call-update) | async-done | bytes 4194320 | tf_op jit(solution)/shard_map/all_gather | solution.py:49
  225.7 2.6 select_add_fusion
  228.3 1.9 copy-done
  230.3 0.9 fusion.87
  231.2 11.7 %cholesky.134 = f32[128,128]{1,0:T(8,128)S(1)} custom-call(f32[128,128]{1,0:T(8,128)S(1)} %fusion.87), custom_call_target="Cholesky" | custom-call | tf_op jit(solution)/shard_map/jit(cholesky)/cholesky | solution.py:29
  243.6 0.7 fusion.56
  244.2 9.8 %custom-call.12 = f32[1,128,128]{1,2,0:T(8,128)S(1)} custom-call(f32[1,128,128]{2,1,0:T(8,128)S(1)} %fusion.56), custom_call_target="InvertDiagBlocksLowerTriangular" | custom-call | tf_op jit(solution)/shard_map/triangular_solve/custom-call.0 | solution.py:31
  254.3 1.1 fusion.70
  255.5 1.1 convolution_subtract_fusion.6
  256.9 11.9 %cholesky.145 = f32[128,128]{1,0:T(8,128)S(1)} custom-call(f32[128,128]{1,0:T(8,128)S(1)} %fusion.85), custom_call_target="Cholesky" | custom-call | tf_op jit(solution)/shard_map/jit(cholesky)/cholesky | solution.py:29
  268.8 0.6 compare_reduce_fusion.6
  269.5 0.7 fusion.57
  270.2 9.8 %custom-call.13 = f32[1,128,128]{1,2,0:T(8,128)S(1)} custom-call(f32[1,128,128]{2,1,0:T(8,128)S(1)} %fusion.57), custom_call_target="InvertDiagBlocksLowerTriangular" | custom-call | tf_op jit(solution)/shard_map/triangular_solve/custom-call.0 | solution.py:31
  280.7 1.5 fusion.28
  282.6 1.4 convolution_subtract_fusion.2
  284.1 11.7 %cholesky.156 = f32[128,128]{1,0:T(8,128)S(1)} custom-call(f32[128,128]{1,0:T(8,128)S(1)} %fusion.83), custom_call_target="Cholesky" | custom-call | tf_op jit(solution)/shard_map/jit(cholesky)/cholesky | solution.py:29
  295.8 0.6 compare_reduce_fusion.5
  296.5 0.7 fusion.58
  297.2 9.8 %custom-call.14 = f32[1,128,128]{1,2,0:T(8,128)S(1)} custom-call(f32[1,128,128]{2,1,0:T(8,128)S(1)} %fusion.58), custom_call_target="InvertDiagBlocksLowerTriangular" | custom-call | tf_op jit(solution)/shard_map/triangular_solve/custom-call.0 | solution.py:31
  308.2 12.1 %cholesky.167 = f32[128,128]{1,0:T(8,128)S(1)} custom-call(f32[128,128]{1,0:T(8,128)S(1)} %fusion.81), custom_call_target="Cholesky" | custom-call | tf_op jit(solution)/shard_map/jit(cholesky)/cholesky | solution.py:29
  320.3 0.6 compare_reduce_fusion.4
  320.9 0.7 fusion.59
  321.6 9.8 %custom-call.15 = f32[1,128,128]{1,2,0:T(8,128)S(1)} custom-call(f32[1,128,128]{2,1,0:T(8,128)S(1)} %fusion.59), custom_call_target="InvertDiagBlocksLowerTriangular" | custom-call | tf_op jit(solution)/shard_map/triangular_solve/custom-call.0 | solution.py:31
  332.5 4.7 %fusion.16 = f32[512,512]{1,0:T(8,128)S(1)} fusion(f32[1024,1024]{0,1:T(8,128)} %copy-done, f32[256,256]{1,0:T(8,128)S(1)} %select_maximum_fusion.4, f32[128,128]{1,0:T(8,128)S(1)} %copy.122, f32[128,128]{1,0:T(8,128)S(1)} %convolution_negate_fusion.5, f32[128,256]{1,0:T(8,128)S(1)} %concatenate.78, f32[256,256]{1,0:T(8,128)S(1)} %convolution_negate_fusion.2), kind=kOutput, calls=%fused_computation.32 | convolution fusion | flops 1612185600 | bytes 2883584 | tf_op jit(solution)/shard_map/dot_general | solution.py:23
  337.2 3.1 convolution_subtract_fusion
  340.3 2.0 fusion.98
  342.4 11.7 %cholesky.178 = f32[128,128]{1,0:T(8,128)S(1)} custom-call(f32[128,128]{1,0:T(8,128)S(1)} %fusion.79), custom_call_target="Cholesky" | custom-call | tf_op jit(solution)/shard_map/jit(cholesky)/cholesky | solution.py:29
  354.8 0.7 fusion.60
  355.5 9.8 %custom-call.16 = f32[1,128,128]{1,2,0:T(8,128)S(1)} custom-call(f32[1,128,128]{2,1,0:T(8,128)S(1)} %fusion.60), custom_call_target="InvertDiagBlocksLowerTriangular" | custom-call | tf_op jit(solution)/shard_map/triangular_solve/custom-call.0 | solution.py:31
  366.5 11.7 %cholesky.189 = f32[128,128]{1,0:T(8,128)S(1)} custom-call(f32[128,128]{1,0:T(8,128)S(1)} %fusion.77), custom_call_target="Cholesky" | custom-call | tf_op jit(solution)/shard_map/jit(cholesky)/cholesky | solution.py:29
  378.2 0.6 compare_reduce_fusion.2
  378.9 0.7 fusion.61
  379.5 9.9 %custom-call.17 = f32[1,128,128]{1,2,0:T(8,128)S(1)} custom-call(f32[1,128,128]{2,1,0:T(8,128)S(1)} %fusion.61), custom_call_target="InvertDiagBlocksLowerTriangular" | custom-call | tf_op jit(solution)/shard_map/triangular_solve/custom-call.0 | solution.py:31
  391.7 11.7 %cholesky.200 = f32[128,128]{1,0:T(8,128)S(1)} custom-call(f32[128,128]{1,0:T(8,128)S(1)} %fusion.75), custom_call_target="Cholesky" | custom-call | tf_op jit(solution)/shard_map/jit(cholesky)/cholesky | solution.py:29
  404.1 0.7 fusion.62
  404.8 9.8 %custom-call.18 = f32[1,128,128]{1,2,0:T(8,128)S(1)} custom-call(f32[1,128,128]{2,1,0:T(8,128)S(1)} %fusion.62), custom_call_target="InvertDiagBlocksLowerTriangular" | custom-call | tf_op jit(solution)/shard_map/triangular_solve/custom-call.0 | solution.py:31
  415.8 12.0 %cholesky.211 = f32[128,128]{1,0:T(8,128)S(1)} custom-call(f32[128,128]{1,0:T(8,128)S(1)} %fusion.73), custom_call_target="Cholesky" | custom-call | tf_op jit(solution)/shard_map/jit(cholesky)/cholesky | solution.py:29
  428.4 0.7 fusion.63
  429.1 9.8 %custom-call.19 = f32[1,128,128]{1,2,0:T(8,128)S(1)} custom-call(f32[1,128,128]{2,1,0:T(8,128)S(1)} %fusion.63), custom_call_target="InvertDiagBlocksLowerTriangular" | custom-call | tf_op jit(solution)/shard_map/triangular_solve/custom-call.0 | solution.py:31
  440.0 1.8 fusion.15
  441.9 4.8 %multiply_reduce_fusion = f32[2048]{0:T(1024)S(1)} fusion(bf16[2048,1024]{1,0:T(8,128)(2,1)S(1)} %copy-done.1, bf16[512,512]{1,0:T(8,128)(2,1)S(1)} %get-tuple-element.8, bf16[512,512]{1,0:T(8,128)(2,1)S(1)} %get-tuple-element.6, bf16[512,512]{1,0:T(8,128)(2,1)S(1)} %fusion.15), kind=kOutput, calls=%fused_computation | convolution fusion | flops 4307548160 | bytes 5775360 | tf_op jit(solution)/shard_map/dot_general | solution.py:69
  (77 shorter events, 13.6 us)
Async XLA Ops:
  6.5 219.2 %all-gather.3.cloned.1.call-start = ((), (), s32[]{:S(2)}) async-start(), calls=%async_computation.2 | async-start | bytes 4718592 | tf_op jit(solution)/shard_map/all_gather | solution.py:49
  228.3 1.9 copy-start
  439.3 2.6 copy-start.1
Sparse Core Ops, SparseCore 0:
  168.9 56.7 all-gather.2

commit v2 on v1

--- a/solution.py
+++ b/solution.py
@@ -1,6 +1,8 @@
 import jax
 import jax.numpy as jnp
 from jax import lax
+from jax.experimental import pallas as pl
+from jax.experimental.pallas import tpu as pltpu
 from jax.sharding import PartitionSpec as P
 
 MEAN = 1024
@@ -23,30 +25,63 @@
     return lax.dot_general(a, b, (((1,), (1,)), ((), ())), precision=HI)
 
 
+def _base_kernel(a_ref, o_ref, m_ref):
+    n = a_ref.shape[0]
+    m_ref[:, :n] = a_ref[...]
+    r = lax.broadcasted_iota(jnp.int32, (n, n), 0)
+    c = lax.broadcasted_iota(jnp.int32, (n, n), 1)
+    m_ref[:, n:] = jnp.where(r == c, 1.0, 0.0).astype(jnp.float32)
+
+    def step(k, carry):
+        row = m_ref[pl.ds(k, 1), :]
+        lane = lax.broadcasted_iota(jnp.int32, (1, 2 * n), 1)
+        piv = jnp.sum(jnp.where(lane == k, row, 0.0), axis=1, keepdims=True)
+        s = 1.0 / jnp.sqrt(piv)
+        rk = row * s
+        m = m_ref[...]
+        left_lane = lax.broadcasted_iota(jnp.int32, (n, n), 1)
+        col = jnp.sum(jnp.where(left_lane == k, m[:, :n], 0.0), axis=1, keepdims=True)
+        sub = lax.broadcasted_iota(jnp.int32, (n, 1), 0)
+        mult = jnp.where(sub > k, col * s, 0.0)
+        m_ref[...] = m - mult * rk
+        m_ref[pl.ds(k, 1), :] = rk
+        return carry
+
+    lax.fori_loop(0, n, step, 0)
+    o_ref[...] = m_ref[:, n:]
+
+
+def base_inv(a):
+    n = a.shape[0]
+    return pl.pallas_call(
+        _base_kernel,
+        out_shape=jax.ShapeDtypeStruct((n, n), jnp.float32),
+        scratch_shapes=[pltpu.VMEM((n, 2 * n), jnp.float32)],
+    )(a)
+
+
 def chol_inv(a):
     n = a.shape[0]
     if n <= BASE:
-        lower = jnp.linalg.cholesky(a)
-        eye = jnp.eye(n, dtype=jnp.float32)
-        return lower, lax.linalg.triangular_solve(lower, eye, left_side=True, lower=True)
+        return base_inv(a)
     h = n // 2
-    l11, i11 = chol_inv(a[:h, :h])
+    i11 = chol_inv(a[:h, :h])
     l21 = mmt(a[h:, :h], i11)
-    l22, i22 = chol_inv(a[h:, h:] - mmt(l21, l21))
+    i22 = chol_inv(a[h:, h:] - mmt(l21, l21))
     i21 = -mm(i22, mm(l21, i11))
     z = jnp.zeros((h, n - h), jnp.float32)
-    return jnp.block([[l11, z], [l21, l22]]), jnp.block([[i11, z], [i21, i22]])
+    return jnp.block([[i11, z], [i21, i22]])
 
 
 def all_sum(g):
     n_dev = lax.axis_size("dev")
     n_grp = lax.axis_size("grp")
     rows, cols = g.shape
-    part = lax.all_to_all(g.reshape(n_dev, rows // n_dev, cols), "dev", 0, 0, tiled=False).sum(0)
+    part = lax.all_to_all(g.reshape(n_grp, rows // n_grp, cols), "grp", 0, 0, tiled=False).sum(0)
     piece = rows // (n_dev * n_grp)
-    part = lax.all_to_all(part.reshape(n_grp, piece, cols), "grp", 0, 0, tiled=False).sum(0)
-    part = lax.all_gather(part, "grp", axis=0, tiled=True)
-    return lax.all_gather(part, "dev", axis=0, tiled=True)
+    part = lax.all_to_all(part.reshape(n_dev, piece, cols), "dev", 0, 0, tiled=False).sum(0)
+    part = lax.all_gather(part, "dev", axis=0, tiled=True)
+    return lax.all_gather(part, "grp", axis=0, tiled=True)
 
 
 def shards(rows, lengths, sketch_block, sketch_sign):
@@ -63,7 +98,7 @@
     gram_matrix = all_sum(add_gram(sketched))
     ridge_value = float(lax.axis_size("grp") * lax.axis_size("dev") * MEAN)
     identity_matrix = jnp.eye(features, dtype=jnp.float32)
-    _, inverse = chol_inv(gram_matrix + ridge_value * identity_matrix)
+    inverse = chol_inv(gram_matrix + ridge_value * identity_matrix)
     weight = inverse.T.astype(jnp.bfloat16)
     factor = ridge_value / features
     projected = jnp.dot(rows, weight, preferred_element_type=jnp.float32)

time: 460 us -> 361 us (0.78)
  other arithmetic: 191 us -> 9.04 us
  Pallas kernels: 0 us -> 129 us
  blocking collectives: 146 us -> 99.9 us
  matrix products: 40.9 us -> 53.2 us
  waiting for transfers between devices: 56.9 us -> 45.5 us
    another operation x41 -> x1, other arithmetic: 184 us -> 0.93 us  [the longest x24 99.9 us: chol_inv(): lower = jnp.linalg.cholesky(a)]
    pallas_call x0 -> x8, Pallas kernels: none -> 129 us  [base_inv(): pl.pallas_call(_base_kernel, out_shape=jax.ShapeDtypeStruct((n, n), jnp.f...]
    all_to_all x2, blocking collectives: 123 us -> 75.2 us  [the longest x1 57.4 us: all_sum(): lax.all_to_all(g.reshape(n_grp, rows // n_grp, cols), 'grp', 0, 0, tiled=...]
    all_gather x1, waiting for transfers between devices: 56.9 us -> 45.5 us  [all_sum(): return lax.all_gather(part, 'grp', axis=0, tiled=True)]
    dot_general x14, matrix products: 7.32 us -> 18 us  [mm(): return jnp.dot(a, b, precision=HI)]
where the time goes in v2:
time: 361 us; the launch traced here: 358 us
  Pallas kernels  129 us (36%)
  blocking collectives  99.9 us (28%)
  matrix products  53.2 us (15%)
  waiting for transfers between devices  45.5 us (13%)
  between operations  14.3 us (4%)
  other arithmetic  9.04 us (3%)
  local copies, waits for them, and re-layouts  6.84 us (2%)
    pallas_call x8, Pallas kernels, base_inv(): pl.pallas_call(_base_kernel, out_shape=jax.ShapeDtypeStruct((n, n), jnp.f...  129 us
    all_to_all x1, blocking collectives, all_sum(): lax.all_to_all(g.reshape(n_grp, rows // n_grp, cols), 'grp', 0, 0, tiled=...  57.4 us
    all_gather x1, waiting for transfers between devices, all_sum(): return lax.all_gather(part, 'grp', axis=0, tiled=True)  45.5 us
    all_gather x1, blocking collectives, all_sum(): part = lax.all_gather(part, 'dev', axis=0, tiled=True)  24.8 us
    dot_general x14, matrix products, mmt(): return lax.dot_general(a, b, (((1,), (1,)), ((), ())), precision=HI)  19.4 us
    dot_general x14, matrix products, mm(): return jnp.dot(a, b, precision=HI)  18 us
    all_to_all x1, blocking collectives, all_sum(): lax.all_to_all(part.reshape(n_dev, piece, cols), 'dev', 0, 0, tiled=False)  17.8 us
    dot_general x1, matrix products, add_gram(): lax.dot_general(row_piece, row_piece, (((0,), (0,)), ((), ())), preferred...  11 us
  transfers between devices with their start and end apart: 1, of which 1 were waited for; matrix products, arithmetic and copies ran while one was open for 0% of the time, Pallas kernels for 0%

profile of v2, /device:TPU:2, one launch (start us, length us, event | category | flops | bytes accessed | tf_op | source)
XLA Modules:
  0.0 358.2 jit_solution(2615929930726334836)
XLA Ops:
  7.9 11.0 %fusion.21 = f32[1024,1024]{1,0:T(8,128)} fusion(bf16[2048,1024]{1,0:T(8,128)(2,1)} %param.4, s32[2048]{0:T(1024)} %param.6, bf16[2048]{0:T(1024)(128)(2,1)S(1)} %select_convert_fusion), kind=kOutput, calls=%fused_computation.38 | convolution fusion | flops 3223846912 | bytes 8400896 | tf_op jit(solution)/shard_map/dot_general | solution.py:15
  18.9 57.4 %all_to_all.10 = f32[32,32,1024]{2,1,0:T(8,128)} all-to-all(f32[32,32,1024]{2,1,0:T(8,128)} %bitcast.47), channel_id=1, replica_groups=mesh['grp'=32,'dev'=8] {'grp'}, dimensions={0} | all-to-all | bytes 8388608 | tf_op jit(solution)/shard_map/all_to_all | solution.py:80
  76.3 2.4 reduce_sum.27
  78.8 17.8 %all_to_all.11 = f32[8,4,1024]{2,1,0:T(4,128)S(1)} all-to-all(f32[8,4,1024]{2,1,0:T(4,128)S(1)} %reshape.13), channel_id=1, replica_groups=mesh['grp'=32,'dev'=8] {'dev'}, dimensions={0} | all-to-all | bytes 262144 | tf_op jit(solution)/shard_map/all_to_all | solution.py:82
  96.6 24.8 %all-gather = f32[8,4,1024]{2,1,0:T(4,128)S(1)} all-gather(f32[1,4,1024]{2,1,0:T(4,128)S(1)} %bitcast.48), channel_id=1, replica_groups=mesh['grp'=32,'dev'=8] {'dev'}, dimensions={0}, use_global_device_ids=true | all-gather | bytes 147456 | tf_op jit(solution)/shard_map/all_gather | solution.py:83
  122.1 45.5 %all-gather.3.cloned.1.call-done = f32[1024,1024]{1,0:T(8,128)} async-done(((f32[32,1024]{1,0:T(8,128)}), f32[1024,1024]{1,0:T(8,128)}) %all-gather.3.cloned.1.call-update) | async-done | bytes 4194320 | tf_op jit(solution)/shard_map/all_gather | solution.py:84
  167.6 2.6 select_add_fusion
  170.1 1.9 copy-done
  172.7 16.1 %shard_map.46 = f32[128,128]{1,0:T(8,128)} custom-call(f32[128,128]{1,0:T(8,128)} %slice.84.a_ref), custom_call_target="tpu_custom_call" | custom-call | tf_op jit(solution)/shard_map/pallas_call | solution.py:56
  188.8 1.1 fusion.46
  190.0 1.0 fusion.62
  191.0 1.7 convolution_subtract_fusion.6.a_ref
  192.7 16.1 %shard_map.47 = f32[128,128]{1,0:T(8,128)} custom-call(f32[128,128]{1,0:T(8,128)} %convolution_subtract_fusion.6.a_ref), custom_call_target="tpu_custom_call" | custom-call | tf_op jit(solution)/shard_map/pallas_call | solution.py:56
  208.9 1.0 convolution_negate_fusion.6
  209.9 0.9 select_maximum_fusion.4
  210.8 1.4 fusion.28
  212.2 1.2 fusion.60
  213.4 1.4 convolution_subtract_fusion.2
  215.4 16.1 %shard_map.48 = f32[128,128]{1,0:T(8,128)} custom-call(f32[128,128]{1,0:T(8,128)} %slice.89.a_ref), custom_call_target="tpu_custom_call" | custom-call | tf_op jit(solution)/shard_map/pallas_call | solution.py:56
  231.6 1.1 fusion.44
  232.7 0.9 convolution_subtract_fusion.5.a_ref
  233.6 1.0 fusion.63
  234.6 0.9 concatenate.78
  235.5 16.1 %shard_map.49 = f32[128,128]{1,0:T(8,128)} custom-call(f32[128,128]{1,0:T(8,128)} %convolution_subtract_fusion.5.a_ref), custom_call_target="tpu_custom_call" | custom-call | tf_op jit(solution)/shard_map/pallas_call | solution.py:56
  251.6 1.0 convolution_negate_fusion.5
  252.7 1.2 convolution_negate_fusion.2
  253.9 3.1 fusion.16
  257.0 3.1 convolution_subtract_fusion
  260.1 1.8 fusion.58
  262.5 16.1 %shard_map.50 = f32[128,128]{1,0:T(8,128)} custom-call(f32[128,128]{1,0:T(8,128)} %slice.94.a_ref), custom_call_target="tpu_custom_call" | custom-call | tf_op jit(solution)/shard_map/pallas_call | solution.py:56
  278.7 1.1 fusion.42
  279.8 1.0 fusion.64
  280.8 0.9 convolution_subtract_fusion.4.a_ref
  281.7 16.1 %shard_map.51 = f32[128,128]{1,0:T(8,128)} custom-call(f32[128,128]{1,0:T(8,128)} %convolution_subtract_fusion.4.a_ref), custom_call_target="tpu_custom_call" | custom-call | tf_op jit(solution)/shard_map/pallas_call | solution.py:56
  297.9 1.0 convolution_negate_fusion.4
  298.9 1.3 fusion.26
  300.6 1.2 fusion.61
  301.9 0.9 select_maximum_fusion.3
  303.4 16.1 %shard_map.52 = f32[128,128]{1,0:T(8,128)} custom-call(f32[128,128]{1,0:T(8,128)} %slice.99.a_ref), custom_call_target="tpu_custom_call" | custom-call | tf_op jit(solution)/shard_map/pallas_call | solution.py:56
  319.5 1.1 fusion.40
  320.6 0.9 convolution_subtract_fusion.3.a_ref
  321.5 1.0 fusion.65
  323.4 16.3 %shard_map.53 = f32[128,128]{1,0:T(8,128)} custom-call(f32[128,128]{1,0:T(8,128)} %convolution_subtract_fusion.3.a_ref), custom_call_target="tpu_custom_call" | custom-call | tf_op jit(solution)/shard_map/pallas_call | solution.py:56
  339.8 1.2 convolution_negate_fusion.3
  341.0 1.3 convolution_negate_fusion.1
  342.3 0.9 fusion.25
  343.2 2.7 fusion.15
  345.9 4.8 %multiply_reduce_fusion = f32[2048]{0:T(1024)S(1)} fusion(bf16[2048,1024]{1,0:T(8,128)(2,1)S(1)} %copy-done.2, bf16[512,512]{1,0:T(8,128)(2,1)S(1)} %get-tuple-element.6, bf16[512,512]{1,0:T(8,128)(2,1)S(1)} %get-tuple-element.5, bf16[512,512]{1,0:T(8,128)(2,1)S(1)} %fusion.15), kind=kOutput, calls=%fused_computation | convolution fusion | flops 4307548160 | bytes 5775360 | tf_op jit(solution)/shard_map/dot_general | solution.py:104
  (18 shorter events, 5.8 us)
Async XLA Ops:
  6.5 161.0 %all-gather.3.cloned.1.call-start = ((), (), s32[]{:S(2)}) async-start(), calls=%async_computation.2 | async-start | bytes 4325376 | tf_op jit(solution)/shard_map/all_gather | solution.py:84
  170.1 1.9 copy-start
  253.9 6.2 %copy-start.1 = (f32[128,128]{1,0:T(8,128)S(1)}, f32[128,128]{1,0:T(8,128)}, u32[]{:S(2)}) copy-start(f32[128,128]{1,0:T(8,128)} %shard_map.49) | copy-start | bytes 196612
  339.8 6.1 %copy-start.2 = (bf16[2048,1024]{1,0:T(8,128)(2,1)S(1)}, bf16[2048,1024]{1,0:T(8,128)(2,1)}, u32[]{:S(2)}) copy-start(bf16[2048,1024]{1,0:T(8,128)(2,1)} %param.4) | copy-start | bytes 12582916
Sparse Core Ops, SparseCore 0:
  122.2 45.3 all-gather.2

commit v3 on v2

--- a/solution.py
+++ b/solution.py
@@ -8,6 +8,7 @@
 MEAN = 1024
 SK_DEV = 512
 BASE = 128
+GROUP = 8
 HI = lax.Precision.HIGHEST
 
 
@@ -32,22 +33,26 @@
     c = lax.broadcasted_iota(jnp.int32, (n, n), 1)
     m_ref[:, n:] = jnp.where(r == c, 1.0, 0.0).astype(jnp.float32)
 
-    def step(k, carry):
-        row = m_ref[pl.ds(k, 1), :]
-        lane = lax.broadcasted_iota(jnp.int32, (1, 2 * n), 1)
-        piv = jnp.sum(jnp.where(lane == k, row, 0.0), axis=1, keepdims=True)
-        s = 1.0 / jnp.sqrt(piv)
-        rk = row * s
-        m = m_ref[...]
-        left_lane = lax.broadcasted_iota(jnp.int32, (n, n), 1)
-        col = jnp.sum(jnp.where(left_lane == k, m[:, :n], 0.0), axis=1, keepdims=True)
-        sub = lax.broadcasted_iota(jnp.int32, (n, 1), 0)
-        mult = jnp.where(sub > k, col * s, 0.0)
-        m_ref[...] = m - mult * rk
-        m_ref[pl.ds(k, 1), :] = rk
-        return carry
+    def make_step(lo):
+        def step(k, carry):
+            row = m_ref[pl.ds(k, 1), :]
+            lane = lax.broadcasted_iota(jnp.int32, (1, 2 * n), 1)
+            piv = jnp.sum(jnp.where(lane == k, row, 0.0), axis=1, keepdims=True)
+            s = lax.rsqrt(piv)
+            rk = row * s
+            m = m_ref[lo:, :]
+            left_lane = lax.broadcasted_iota(jnp.int32, (n - lo, n), 1)
+            col = jnp.sum(jnp.where(left_lane == k, m[:, :n], 0.0), axis=1, keepdims=True)
+            sub = lax.broadcasted_iota(jnp.int32, (n - lo, 1), 0) + lo
+            mult = jnp.where(sub > k, col * s, 0.0)
+            m_ref[lo:, :] = m - mult * rk
+            m_ref[pl.ds(k, 1), :] = rk
+            return carry
 
-    lax.fori_loop(0, n, step, 0)
+        return step
+
+    for g in range(n // GROUP):
+        lax.fori_loop(g * GROUP, (g + 1) * GROUP, make_step(g * GROUP), 0)
     o_ref[...] = m_ref[:, n:]
 
 
@@ -95,10 +100,18 @@
         jnp.bfloat16
     ) * row_sign[None, :]
     sketched = jnp.dot(picker, rows, preferred_element_type=jnp.float32).astype(jnp.bfloat16)
-    gram_matrix = all_sum(add_gram(sketched))
+    h = features // 2
+    gram_left = all_sum(lax.dot_general(
+        sketched, sketched[:, :h], (((0,), (0,)), ((), ())), preferred_element_type=jnp.float32
+    ))
+    gram_corner = all_sum(add_gram(sketched[:, h:]))
     ridge_value = float(lax.axis_size("grp") * lax.axis_size("dev") * MEAN)
-    identity_matrix = jnp.eye(features, dtype=jnp.float32)
-    inverse = chol_inv(gram_matrix + ridge_value * identity_matrix)
+    ridge = ridge_value * jnp.eye(h, dtype=jnp.float32)
+    i11 = chol_inv(gram_left[:h] + ridge)
+    l21 = mmt(gram_left[h:], i11)
+    i22 = chol_inv(gram_corner + ridge - mmt(l21, l21))
+    i21 = -mm(i22, mm(l21, i11))
+    inverse = jnp.block([[i11, jnp.zeros((h, h), jnp.float32)], [i21, i22]])
     weight = inverse.T.astype(jnp.bfloat16)
     factor = ridge_value / features
     projected = jnp.dot(rows, weight, preferred_element_type=jnp.float32)

time: 361 us -> 320 us (0.89)
  waiting for transfers between devices: 45.5 us -> 0.06 us
  blocking collectives: 99.9 us -> 133 us
  Pallas kernels: 129 us -> 115 us
  matrix products: 53.2 us -> 46.9 us
  other arithmetic: 9.04 us -> 4.02 us
    all_gather x1 -> x2, waiting for transfers between devices: 45.5 us -> 0.02 us  [all_sum(): return lax.all_gather(part, 'grp', axis=0, tiled=True)]
    all_gather x1 -> x2, blocking collectives: 24.8 us -> 49.4 us  [all_sum(): part = lax.all_gather(part, 'dev', axis=0, tiled=True)]
    pallas_call x8, Pallas kernels: 129 us -> 115 us  [base_inv(): pl.pallas_call(_base_kernel, out_shape=jax.ShapeDtypeStruct((n, n), jnp.f...]
    dot_general x1, matrix products: 11 us -> 0.46 us  [add_gram(): lax.dot_general(row_piece, row_piece, (((0,), (0,)), ((), ())), preferred...]
    all_to_all x1 -> x2, blocking collectives: 17.8 us -> 27.1 us  [all_sum(): lax.all_to_all(part.reshape(n_dev, piece, cols), 'dev', 0, 0, tiled=False)]
    dot_general x0 -> x2, matrix products: none -> 5.27 us  [the longest x1 4.53 us: shards(): jnp.dot(picker, rows, preferred_element_type=jnp.float32)]
    all_to_all x1 -> x2, blocking collectives: 57.4 us -> 56 us  [all_sum(): lax.all_to_all(g.reshape(n_grp, rows // n_grp, cols), 'grp', 0, 0, tiled=...]
  transfers between devices with their start and end apart: 1 -> 2, of which waited for: 1 -> 0; matrix products, arithmetic and copies ran while one was open for 0% -> 7% of each run, Pallas kernels for 0% -> 18%
where the time goes in v3:
time: 320 us; the launch traced here: 318 us
  blocking collectives  133 us (42%)
  Pallas kernels  115 us (36%)
  matrix products  46.9 us (15%)
  between operations  14.3 us (4%)
  local copies, waits for them, and re-layouts  5.54 us (2%)
  other arithmetic  4.02 us (1%)
    pallas_call x8, Pallas kernels, base_inv(): pl.pallas_call(_base_kernel, out_shape=jax.ShapeDtypeStruct((n, n), jnp.f...  115 us
    all_to_all x2, blocking collectives, all_sum(): lax.all_to_all(g.reshape(n_grp, rows // n_grp, cols), 'grp', 0, 0, tiled=...  56 us
    all_gather x2, blocking collectives, all_sum(): part = lax.all_gather(part, 'dev', axis=0, tiled=True)  49.4 us
    all_to_all x2, blocking collectives, all_sum(): lax.all_to_all(part.reshape(n_dev, piece, cols), 'dev', 0, 0, tiled=False)  27.1 us
    dot_general x14, matrix products, mm(): return jnp.dot(a, b, precision=HI)  18.7 us
    dot_general x14, matrix products, mmt(): return lax.dot_general(a, b, (((1,), (1,)), ((), ())), precision=HI)  17.7 us
  transfers between devices with their start and end apart: 2, of which 0 were waited for; matrix products, arithmetic and copies ran while one was open for 7% of the time, Pallas kernels for 18%

profile of v3, /device:TPU:2, one launch (start us, length us, event | category | flops | bytes accessed | tf_op | source)
XLA Modules:
  0.0 318.1 jit_solution(8958925711472347836)
XLA Ops:
  7.2 0.7 select_convert_fusion
  7.9 4.5 %fusion.12 = bf16[512,1024]{1,0:T(8,128)(2,1)S(1)} fusion(bf16[2048,1024]{1,0:T(8,128)(2,1)} %param.4, s32[2048]{0:T(1024)} %param.6, bf16[2048]{0:T(1024)(128)(2,1)S(1)} %select_convert_fusion), kind=kOutput, calls=%fused_computation.13 | convolution fusion | flops 2150105088 | bytes 5255168 | tf_op jit(solution)/shard_map/dot_general | solution.py:102
  12.4 0.7 fusion.23
  13.2 34.6 %all_to_all.20 = f32[32,32,512]{2,1,0:T(8,128)S(1)} all-to-all(f32[32,32,512]{2,1,0:T(8,128)S(1)} %bitcast.50), channel_id=1, replica_groups=mesh['grp'=32,'dev'=8] {'grp'}, dimensions={0} | all-to-all | bytes 4194304 | tf_op jit(solution)/shard_map/all_to_all | solution.py:85
  48.0 16.6 %all_to_all.21 = f32[8,4,512]{2,1,0:T(4,128)S(1)} all-to-all(f32[8,4,512]{2,1,0:T(4,128)S(1)} %reshape.19), channel_id=1, replica_groups=mesh['grp'=32,'dev'=8] {'dev'}, dimensions={0} | all-to-all | bytes 131072 | tf_op jit(solution)/shard_map/all_to_all | solution.py:87
  64.7 24.6 %all-gather = f32[8,4,512]{2,1,0:T(4,128)S(1)} all-gather(f32[1,4,512]{2,1,0:T(4,128)S(1)} %bitcast.52), channel_id=1, replica_groups=mesh['grp'=32,'dev'=8] {'dev'}, dimensions={0}, use_global_device_ids=true | all-gather | bytes 73728 | tf_op jit(solution)/shard_map/all_gather | solution.py:88
  89.3 0.6 reshape.23
  90.4 21.4 %all_to_all.22 = f32[32,16,512]{2,1,0:T(8,128)S(1)} all-to-all(f32[32,16,512]{2,1,0:T(8,128)S(1)} %bitcast.51), channel_id=1, replica_groups=mesh['grp'=32,'dev'=8] {'grp'}, dimensions={0} | all-to-all | bytes 2097152 | tf_op jit(solution)/shard_map/all_to_all | solution.py:85
  111.9 10.4 %all_to_all.23 = f32[8,2,512]{2,1,0:T(2,128)S(1)} all-to-all(f32[8,2,512]{2,1,0:T(2,128)S(1)} %reshape.21), channel_id=1, replica_groups=mesh['grp'=32,'dev'=8] {'dev'}, dimensions={0} | all-to-all | bytes 65536 | tf_op jit(solution)/shard_map/all_to_all | solution.py:87
  122.4 24.8 %all-gather.1 = f32[8,2,512]{2,1,0:T(2,128)S(1)} all-gather(f32[1,2,512]{2,1,0:T(2,128)S(1)} %bitcast.53), channel_id=1, replica_groups=mesh['grp'=32,'dev'=8] {'dev'}, dimensions={0}, use_global_device_ids=true | all-gather | bytes 36864 | tf_op jit(solution)/shard_map/all_gather | solution.py:88
  147.9 1.3 select_add_fusion.1
  149.9 14.3 %shard_map.46 = f32[128,128]{1,0:T(8,128)} custom-call(f32[128,128]{1,0:T(8,128)} %slice.90.a_ref), custom_call_target="tpu_custom_call" | custom-call | tf_op jit(solution)/shard_map/pallas_call | solution.py:61
  164.2 1.2 fusion.46
  165.4 1.0 fusion.61
  166.4 0.9 convolution_subtract_fusion.6.a_ref
  167.3 14.3 %shard_map.47 = f32[128,128]{1,0:T(8,128)} custom-call(f32[128,128]{1,0:T(8,128)} %convolution_subtract_fusion.6.a_ref), custom_call_target="tpu_custom_call" | custom-call | tf_op jit(solution)/shard_map/pallas_call | solution.py:61
  181.6 1.1 convolution_negate_fusion.6
  182.8 1.3 fusion.28
  185.1 14.3 %shard_map.48 = f32[128,128]{1,0:T(8,128)} custom-call(f32[128,128]{1,0:T(8,128)} %slice.95.a_ref), custom_call_target="tpu_custom_call" | custom-call | tf_op jit(solution)/shard_map/pallas_call | solution.py:61
  199.4 1.1 fusion.44
  200.5 0.9 concatenate.78
  201.4 0.9 convolution_subtract_fusion.5.a_ref
  202.3 14.3 %shard_map.49 = f32[128,128]{1,0:T(8,128)} custom-call(f32[128,128]{1,0:T(8,128)} %convolution_subtract_fusion.5.a_ref), custom_call_target="tpu_custom_call" | custom-call | tf_op jit(solution)/shard_map/pallas_call | solution.py:61
  216.6 1.1 fusion.62
  217.7 1.0 convolution_negate_fusion.5
  219.1 1.2 convolution_negate_fusion.2
  220.4 3.1 fusion.16
  223.5 2.8 fusion.57
  226.3 3.1 convolution_subtract_fusion
  230.0 14.3 %shard_map.50 = f32[128,128]{1,0:T(8,128)} custom-call(f32[128,128]{1,0:T(8,128)} %slice.100.a_ref), custom_call_target="tpu_custom_call" | custom-call | tf_op jit(solution)/shard_map/pallas_call | solution.py:61
  244.3 1.2 fusion.42
  245.5 1.0 fusion.63
  246.6 0.9 convolution_subtract_fusion.4.a_ref
  247.5 14.4 %shard_map.51 = f32[128,128]{1,0:T(8,128)} custom-call(f32[128,128]{1,0:T(8,128)} %convolution_subtract_fusion.4.a_ref), custom_call_target="tpu_custom_call" | custom-call | tf_op jit(solution)/shard_map/pallas_call | solution.py:61
  261.9 1.1 convolution_negate_fusion.4
  263.0 1.3 fusion.26
  264.7 1.2 fusion.60
  266.6 14.3 %shard_map.52 = f32[128,128]{1,0:T(8,128)} custom-call(f32[128,128]{1,0:T(8,128)} %slice.105.a_ref), custom_call_target="tpu_custom_call" | custom-call | tf_op jit(solution)/shard_map/pallas_call | solution.py:61
  280.9 1.1 fusion.40
  282.0 0.9 convolution_subtract_fusion.3.a_ref
  282.9 1.0 fusion.64
  284.0 0.9 concatenate.88
  284.8 14.3 %shard_map.53 = f32[128,128]{1,0:T(8,128)} custom-call(f32[128,128]{1,0:T(8,128)} %convolution_subtract_fusion.3.a_ref), custom_call_target="tpu_custom_call" | custom-call | tf_op jit(solution)/shard_map/pallas_call | solution.py:61
  299.2 1.1 convolution_negate_fusion.3
  300.3 1.2 convolution_negate_fusion.1
  301.5 1.0 fusion.25
  302.6 3.3 %fusion.15 = bf16[512,512]{1,0:T(8,128)(2,1)S(1)} fusion(f32[512,512]{1,0:T(8,128)} %fusion.57, f32[256,256]{1,0:T(8,128)S(1)} %select_maximum_fusion.3, f32[128,128]{1,0:T(8,128)S(1)} %copy-done.5, f32[128,128]{1,0:T(8,128)S(1)} %convolution_negate_fusion.3, f32[128,256]{1,0:T(8,128)S(1)} %concatenate.88, f32[256,256]{1,0:T(8,128)S(1)} %convolution_negate_fusion.1), kind=kOutput, calls=%fused_computation.18 | convolution fusion | flops 1612709888 | bytes 2359296 | tf_op jit(solution)/shard_map/dot_general | solution.py:22
  305.9 4.8 %multiply_reduce_fusion = f32[2048]{0:T(1024)S(1)} fusion(bf16[2048,1024]{1,0:T(8,128)(2,1)S(1)} %copy-done.6, bf16[512,512]{1,0:T(8,128)(2,1)S(1)} %fusion.58, bf16[512,512]{1,0:T(8,128)(2,1)S(1)} %fusion.25, bf16[512,512]{1,0:T(8,128)(2,1)S(1)} %fusion.15), kind=kOutput, calls=%fused_computation | convolution fusion | flops 4307548160 | bytes 5775360 | tf_op jit(solution)/shard_map/dot_general | solution.py:117
  (39 shorter events, 5.9 us)
Async XLA Ops:
  6.5 141.4 %all-gather.5.cloned.1.call-start = ((), (), s32[]{:S(2)}) async-start(), calls=%async_computation.4 | async-start | bytes 2162688 | tf_op jit(solution)/shard_map/all_gather | solution.py:89
  89.9 136.4 %all-gather.7.cloned.1.call-start = ((), (), s32[]{:S(2)}) async-start(), calls=%async_computation.5 | async-start | bytes 1081344 | tf_op jit(solution)/shard_map/all_gather | solution.py:89
  164.2 52.4 %copy-start = (f32[128,128]{1,0:T(8,128)S(1)}, f32[128,128]{1,0:T(8,128)}, u32[]{:S(2)}) copy-start(f32[128,128]{1,0:T(8,128)} %shard_map.46) | copy-start | bytes 196612
  181.6 35.0 %copy-start.2 = (f32[128,128]{1,0:T(8,128)S(1)}, f32[128,128]{1,0:T(8,128)}, u32[]{:S(2)}) copy-start(f32[128,128]{1,0:T(8,128)} %shard_map.47) | copy-start | bytes 196612
  216.6 3.8 %copy-start.4 = (f32[128,128]{1,0:T(8,128)S(1)}, f32[128,128]{1,0:T(8,128)}, u32[]{:S(2)}) copy-start(f32[128,128]{1,0:T(8,128)} %shard_map.49) | copy-start | bytes 196612
  244.3 20.4 %copy-start.1 = (f32[128,128]{1,0:T(8,128)S(1)}, f32[128,128]{1,0:T(8,128)}, u32[]{:S(2)}) copy-start(f32[128,128]{1,0:T(8,128)} %shard_map.50) | copy-start | bytes 196612
  261.9 4.1 %copy-start.3 = (f32[128,128]{1,0:T(8,128)S(1)}, f32[128,128]{1,0:T(8,128)}, u32[]{:S(2)}) copy-start(f32[128,128]{1,0:T(8,128)} %shard_map.51) | copy-start | bytes 196612
  299.2 3.4 %copy-start.5 = (f32[128,128]{1,0:T(8,128)S(1)}, f32[128,128]{1,0:T(8,128)}, u32[]{:S(2)}) copy-start(f32[128,128]{1,0:T(8,128)} %shard_map.53) | copy-start | bytes 196612
  301.5 4.4 %copy-start.6 = (bf16[2048,1024]{1,0:T(8,128)(2,1)S(1)}, bf16[2048,1024]{1,0:T(8,128)(2,1)}, u32[]{:S(2)}) copy-start(bf16[2048,1024]{1,0:T(8,128)(2,1)} %param.4) | copy-start | bytes 12582916
Sparse Core Ops, SparseCore 0:
  90.0 45.1 all-gather.4
  148.0 41.8 all-gather.6

commit v4 on v3

--- a/solution.py
+++ b/solution.py
@@ -85,7 +85,8 @@
     part = lax.all_to_all(g.reshape(n_grp, rows // n_grp, cols), "grp", 0, 0, tiled=False).sum(0)
     piece = rows // (n_dev * n_grp)
     part = lax.all_to_all(part.reshape(n_dev, piece, cols), "dev", 0, 0, tiled=False).sum(0)
-    part = lax.all_gather(part, "dev", axis=0, tiled=True)
+    part = jnp.broadcast_to(part[None], (n_dev,) + part.shape)
+    part = lax.all_to_all(part, "dev", 0, 0, tiled=False).reshape(n_dev * piece, cols)
     return lax.all_gather(part, "grp", axis=0, tiled=True)
 
 

time: 320 us -> 294 us (0.919)
  blocking collectives: 133 us -> 104 us
    all_gather x2 -> x0, blocking collectives: 49.4 us -> none  [all_sum(): part = lax.all_gather(part, 'dev', axis=0, tiled=True)]
    all_to_all x0 -> x2, blocking collectives: none -> 21.1 us  [all_sum(): lax.all_to_all(part, 'dev', 0, 0, tiled=False).reshape(n_dev * piece, cols)]
  transfers between devices with their start and end apart: 2 -> 2, of which waited for: 0 -> 1; matrix products, arithmetic and copies ran while one was open for 7% -> 8% of each run, Pallas kernels for 18% -> 20%
where the time goes in v4:
time: 294 us; the launch traced here: 291 us
  Pallas kernels  115 us (39%)
  blocking collectives  104 us (35%)
  matrix products  46.9 us (16%)
  between operations  14.4 us (5%)
  local copies, waits for them, and re-layouts  5.56 us (2%)
  other arithmetic  4.02 us (1%)
    pallas_call x8, Pallas kernels, base_inv(): pl.pallas_call(_base_kernel, out_shape=jax.ShapeDtypeStruct((n, n), jnp.f...  115 us
    all_to_all x2, blocking collectives, all_sum(): lax.all_to_all(g.reshape(n_grp, rows // n_grp, cols), 'grp', 0, 0, tiled=...  56.2 us
    all_to_all x2, blocking collectives, all_sum(): lax.all_to_all(part.reshape(n_dev, piece, cols), 'dev', 0, 0, tiled=False)  27 us
    all_to_all x2, blocking collectives, all_sum(): lax.all_to_all(part, 'dev', 0, 0, tiled=False).reshape(n_dev * piece, cols)  21.1 us
    dot_general x14, matrix products, mm(): return jnp.dot(a, b, precision=HI)  18.7 us
    dot_general x14, matrix products, mmt(): return lax.dot_general(a, b, (((1,), (1,)), ((), ())), precision=HI)  17.7 us
  transfers between devices with their start and end apart: 2, of which 1 were waited for; matrix products, arithmetic and copies ran while one was open for 8% of the time, Pallas kernels for 20%

profile of v4, /device:TPU:2, one launch (start us, length us, event | category | flops | bytes accessed | tf_op | source)
XLA Modules:
  0.0 290.8 jit_solution(16801884651595767296)
XLA Ops:
  7.2 0.7 select_convert_fusion
  7.9 4.5 %fusion.12 = bf16[512,1024]{1,0:T(8,128)(2,1)S(1)} fusion(bf16[2048,1024]{1,0:T(8,128)(2,1)} %param.4, s32[2048]{0:T(1024)} %param.6, bf16[2048]{0:T(1024)(128)(2,1)S(1)} %select_convert_fusion), kind=kOutput, calls=%fused_computation.13 | convolution fusion | flops 2150105088 | bytes 5255168 | tf_op jit(solution)/shard_map/dot_general | solution.py:103
  12.4 0.7 fusion.23
  13.2 34.6 %all_to_all.30 = f32[32,32,512]{2,1,0:T(8,128)S(1)} all-to-all(f32[32,32,512]{2,1,0:T(8,128)S(1)} %bitcast.48), channel_id=1, replica_groups=mesh['grp'=32,'dev'=8] {'grp'}, dimensions={0} | all-to-all | bytes 4194304 | tf_op jit(solution)/shard_map/all_to_all | solution.py:85
  48.0 16.6 %all_to_all.31 = f32[8,4,512]{2,1,0:T(4,128)S(1)} all-to-all(f32[8,4,512]{2,1,0:T(4,128)S(1)} %reshape.27), channel_id=1, replica_groups=mesh['grp'=32,'dev'=8] {'dev'}, dimensions={0} | all-to-all | bytes 131072 | tf_op jit(solution)/shard_map/all_to_all | solution.py:87
  64.7 10.7 %all_to_all.32 = f32[8,4,512]{2,1,0:T(4,128)S(1)} all-to-all(f32[8,4,512]{2,1,0:T(4,128)S(1)} %broadcast_in_dim.12), channel_id=1, replica_groups=mesh['grp'=32,'dev'=8] {'dev'}, dimensions={0} | all-to-all | bytes 131072 | tf_op jit(solution)/shard_map/all_to_all | solution.py:89
  76.6 21.6 %all_to_all.33 = f32[32,16,512]{2,1,0:T(8,128)S(1)} all-to-all(f32[32,16,512]{2,1,0:T(8,128)S(1)} %bitcast.49), channel_id=1, replica_groups=mesh['grp'=32,'dev'=8] {'grp'}, dimensions={0} | all-to-all | bytes 2097152 | tf_op jit(solution)/shard_map/all_to_all | solution.py:85
  98.3 10.4 %all_to_all.34 = f32[8,2,512]{2,1,0:T(2,128)S(1)} all-to-all(f32[8,2,512]{2,1,0:T(2,128)S(1)} %reshape.30), channel_id=1, replica_groups=mesh['grp'=32,'dev'=8] {'dev'}, dimensions={0} | all-to-all | bytes 65536 | tf_op jit(solution)/shard_map/all_to_all | solution.py:87
  108.7 10.4 %all_to_all.35 = f32[8,2,512]{2,1,0:T(2,128)S(1)} all-to-all(f32[8,2,512]{2,1,0:T(2,128)S(1)} %broadcast_in_dim.13), channel_id=1, replica_groups=mesh['grp'=32,'dev'=8] {'dev'}, dimensions={0} | all-to-all | bytes 65536 | tf_op jit(solution)/shard_map/all_to_all | solution.py:89
  119.8 0.8 all-gather.3.cloned.1.call-done
  120.6 1.3 select_add_fusion.1
  122.5 14.3 %shard_map.46 = f32[128,128]{1,0:T(8,128)} custom-call(f32[128,128]{1,0:T(8,128)} %slice.90.a_ref), custom_call_target="tpu_custom_call" | custom-call | tf_op jit(solution)/shard_map/pallas_call | solution.py:61
  136.8 1.2 fusion.46
  138.0 1.0 fusion.61
  139.1 0.9 convolution_subtract_fusion.6.a_ref
  140.0 14.3 %shard_map.47 = f32[128,128]{1,0:T(8,128)} custom-call(f32[128,128]{1,0:T(8,128)} %convolution_subtract_fusion.6.a_ref), custom_call_target="tpu_custom_call" | custom-call | tf_op jit(solution)/shard_map/pallas_call | solution.py:61
  154.3 1.1 convolution_negate_fusion.6
  155.4 1.3 fusion.28
  157.7 14.3 %shard_map.48 = f32[128,128]{1,0:T(8,128)} custom-call(f32[128,128]{1,0:T(8,128)} %slice.95.a_ref), custom_call_target="tpu_custom_call" | custom-call | tf_op jit(solution)/shard_map/pallas_call | solution.py:61
  172.1 1.1 fusion.44
  173.2 0.9 concatenate.78
  174.0 0.9 convolution_subtract_fusion.5.a_ref
  174.9 14.3 %shard_map.49 = f32[128,128]{1,0:T(8,128)} custom-call(f32[128,128]{1,0:T(8,128)} %convolution_subtract_fusion.5.a_ref), custom_call_target="tpu_custom_call" | custom-call | tf_op jit(solution)/shard_map/pallas_call | solution.py:61
  189.3 1.1 fusion.62
  190.3 1.0 convolution_negate_fusion.5
  191.8 1.2 convolution_negate_fusion.2
  193.1 3.1 %fusion.16 = f32[512,512]{1,0:T(8,128)S(1)} fusion(f32[1024,512]{1,0:T(8,128)} %all-gather.3.cloned.1.call-done, f32[256,256]{1,0:T(8,128)S(1)} %select_maximum_fusion.4, f32[128,128]{1,0:T(8,128)S(1)} %copy-done.4, f32[128,128]{1,0:T(8,128)S(1)} %convolution_negate_fusion.5, f32[128,256]{1,0:T(8,128)S(1)} %concatenate.78, ...), kind=kOutput, calls=%fused_computation.32 | convolution fusion | flops 1612185600 | bytes 2883584 | tf_op jit(solution)/shard_map/dot_general | solution.py:26
  196.2 2.8 fusion.57
  198.9 3.1 %convolution_subtract_fusion = f32[512,512]{1,0:T(8,128)S(1)} fusion(f32[512,512]{1,0:T(8,128)S(1)} %fusion.16, f32[512,512]{1,0:T(8,128)} %all-gather.5.cloned.1.call-done), kind=kOutput, calls=%fused_computation.17 | convolution fusion | flops 1611661312 | bytes 3145728 | tf_op jit(solution)/shard_map/dot_general | solution.py:26
  202.7 14.3 %shard_map.50 = f32[128,128]{1,0:T(8,128)} custom-call(f32[128,128]{1,0:T(8,128)} %slice.100.a_ref), custom_call_target="tpu_custom_call" | custom-call | tf_op jit(solution)/shard_map/pallas_call | solution.py:61
  217.0 1.2 fusion.42
  218.2 1.0 fusion.63
  219.2 0.9 convolution_subtract_fusion.4.a_ref
  220.1 14.4 %shard_map.51 = f32[128,128]{1,0:T(8,128)} custom-call(f32[128,128]{1,0:T(8,128)} %convolution_subtract_fusion.4.a_ref), custom_call_target="tpu_custom_call" | custom-call | tf_op jit(solution)/shard_map/pallas_call | solution.py:61
  234.6 1.1 convolution_negate_fusion.4
  235.7 1.3 fusion.26
  237.4 1.2 fusion.60
  239.3 14.3 %shard_map.52 = f32[128,128]{1,0:T(8,128)} custom-call(f32[128,128]{1,0:T(8,128)} %slice.105.a_ref), custom_call_target="tpu_custom_call" | custom-call | tf_op jit(solution)/shard_map/pallas_call | solution.py:61
  253.6 1.1 fusion.40
  254.7 0.9 convolution_subtract_fusion.3.a_ref
  255.6 1.0 fusion.64
  256.6 0.9 concatenate.88
  257.5 14.3 %shard_map.53 = f32[128,128]{1,0:T(8,128)} custom-call(f32[128,128]{1,0:T(8,128)} %convolution_subtract_fusion.3.a_ref), custom_call_target="tpu_custom_call" | custom-call | tf_op jit(solution)/shard_map/pallas_call | solution.py:61
  271.8 1.1 convolution_negate_fusion.3
  272.9 1.2 convolution_negate_fusion.1
  274.2 1.0 fusion.25
  275.2 3.3 %fusion.15 = bf16[512,512]{1,0:T(8,128)(2,1)S(1)} fusion(f32[512,512]{1,0:T(8,128)} %fusion.57, f32[256,256]{1,0:T(8,128)S(1)} %select_maximum_fusion.3, f32[128,128]{1,0:T(8,128)S(1)} %copy-done.5, f32[128,128]{1,0:T(8,128)S(1)} %convolution_negate_fusion.3, f32[128,256]{1,0:T(8,128)S(1)} %concatenate.88, f32[256,256]{1,0:T(8,128)S(1)} %convolution_negate_fusion.1), kind=kOutput, calls=%fused_computation.18 | convolution fusion | flops 1612709888 | bytes 2359296 | tf_op jit(solution)/shard_map/dot_general | solution.py:22
  278.5 4.8 %multiply_reduce_fusion = f32[2048]{0:T(1024)S(1)} fusion(bf16[2048,1024]{1,0:T(8,128)(2,1)S(1)} %copy-done.6, bf16[512,512]{1,0:T(8,128)(2,1)S(1)} %fusion.58, bf16[512,512]{1,0:T(8,128)(2,1)S(1)} %fusion.25, bf16[512,512]{1,0:T(8,128)(2,1)S(1)} %fusion.15), kind=kOutput, calls=%fused_computation | convolution fusion | flops 4307548160 | bytes 5775360 | tf_op jit(solution)/shard_map/dot_general | solution.py:118
  (41 shorter events, 6.5 us)
Async XLA Ops:
  6.5 114.0 %all-gather.3.cloned.1.call-start = ((), (), s32[]{:S(2)}) async-start(), calls=%async_computation.6 | async-start | bytes 2162688 | tf_op jit(solution)/shard_map/all_gather | solution.py:90
  76.1 122.9 %all-gather.5.cloned.1.call-start = ((), (), s32[]{:S(2)}) async-start(), calls=%async_computation.7 | async-start | bytes 1081344 | tf_op jit(solution)/shard_map/all_gather | solution.py:90
  136.8 52.4 %copy-start = (f32[128,128]{1,0:T(8,128)S(1)}, f32[128,128]{1,0:T(8,128)}, u32[]{:S(2)}) copy-start(f32[128,128]{1,0:T(8,128)} %shard_map.46) | copy-start | bytes 196612
  154.3 34.9 %copy-start.2 = (f32[128,128]{1,0:T(8,128)S(1)}, f32[128,128]{1,0:T(8,128)}, u32[]{:S(2)}) copy-start(f32[128,128]{1,0:T(8,128)} %shard_map.47) | copy-start | bytes 196612
  189.2 3.8 %copy-start.4 = (f32[128,128]{1,0:T(8,128)S(1)}, f32[128,128]{1,0:T(8,128)}, u32[]{:S(2)}) copy-start(f32[128,128]{1,0:T(8,128)} %shard_map.49) | copy-start | bytes 196612
  217.0 20.4 %copy-start.1 = (f32[128,128]{1,0:T(8,128)S(1)}, f32[128,128]{1,0:T(8,128)}, u32[]{:S(2)}) copy-start(f32[128,128]{1,0:T(8,128)} %shard_map.50) | copy-start | bytes 196612
  234.6 4.1 %copy-start.3 = (f32[128,128]{1,0:T(8,128)S(1)}, f32[128,128]{1,0:T(8,128)}, u32[]{:S(2)}) copy-start(f32[128,128]{1,0:T(8,128)} %shard_map.51) | copy-start | bytes 196612
  271.8 3.4 %copy-start.5 = (f32[128,128]{1,0:T(8,128)S(1)}, f32[128,128]{1,0:T(8,128)}, u32[]{:S(2)}) copy-start(f32[128,128]{1,0:T(8,128)} %shard_map.53) | copy-start | bytes 196612
  274.2 4.4 %copy-start.6 = (bf16[2048,1024]{1,0:T(8,128)(2,1)S(1)}, bf16[2048,1024]{1,0:T(8,128)(2,1)}, u32[]{:S(2)}) copy-start(bf16[2048,1024]{1,0:T(8,128)(2,1)} %param.4) | copy-start | bytes 12582916
Sparse Core Ops, SparseCore 0:
  76.2 44.2 all-gather.2
  123.1 47.2 all-gather.4

commit v5 on v3

--- a/solution.py
+++ b/solution.py
@@ -78,15 +78,28 @@
     return jnp.block([[i11, z], [i21, i22]])
 
 
-def all_sum(g):
+def all_sum(left, corner):
     n_dev = lax.axis_size("dev")
     n_grp = lax.axis_size("grp")
-    rows, cols = g.shape
-    part = lax.all_to_all(g.reshape(n_grp, rows // n_grp, cols), "grp", 0, 0, tiled=False).sum(0)
-    piece = rows // (n_dev * n_grp)
-    part = lax.all_to_all(part.reshape(n_dev, piece, cols), "dev", 0, 0, tiled=False).sum(0)
-    part = lax.all_gather(part, "dev", axis=0, tiled=True)
-    return lax.all_gather(part, "grp", axis=0, tiled=True)
+    shapes = [x.shape for x in (left, corner)]
+    chunks = [x.shape[0] // n_grp for x in (left, corner)]
+    pieces = [c // n_dev for c in chunks]
+    both = jnp.concatenate(
+        [x.reshape(n_grp, c, x.shape[1]) for x, c in zip((left, corner), chunks)], axis=1
+    )
+    both = lax.all_to_all(both, "grp", 0, 0, tiled=False).sum(0)
+    both = jnp.concatenate(
+        [both[:chunks[0]].reshape(n_dev, pieces[0], -1), both[chunks[0]:].reshape(n_dev, pieces[1], -1)],
+        axis=1,
+    )
+    both = lax.all_to_all(both, "dev", 0, 0, tiled=False).sum(0)
+    both = jnp.broadcast_to(both[None], (n_dev,) + both.shape)
+    both = lax.all_to_all(both, "dev", 0, 0, tiled=False)
+    outs = []
+    for part, piece, shape in ((both[:, :pieces[0]], pieces[0], shapes[0]), (both[:, pieces[0]:], pieces[1], shapes[1])):
+        part = part.reshape(n_dev * piece, shape[1])
+        outs.append(lax.all_gather(part, "grp", axis=0, tiled=True))
+    return outs
 
 
 def shards(rows, lengths, sketch_block, sketch_sign):
@@ -101,10 +114,12 @@
     ) * row_sign[None, :]
     sketched = jnp.dot(picker, rows, preferred_element_type=jnp.float32).astype(jnp.bfloat16)
     h = features // 2
-    gram_left = all_sum(lax.dot_general(
-        sketched, sketched[:, :h], (((0,), (0,)), ((), ())), preferred_element_type=jnp.float32
-    ))
-    gram_corner = all_sum(add_gram(sketched[:, h:]))
+    gram_left, gram_corner = all_sum(
+        lax.dot_general(
+            sketched, sketched[:, :h], (((0,), (0,)), ((), ())), preferred_element_type=jnp.float32
+        ),
+        add_gram(sketched[:, h:]),
+    )
     ridge_value = float(lax.axis_size("grp") * lax.axis_size("dev") * MEAN)
     ridge = ridge_value * jnp.eye(h, dtype=jnp.float32)
     i11 = chol_inv(gram_left[:h] + ridge)

time: 320 us -> 308 us (0.963)
  blocking collectives: 133 us -> 75.1 us
  waiting for transfers between devices: 0.06 us -> 41.7 us
    all_gather x2 -> x0, blocking collectives: 49.4 us -> none  [all_sum(): part = lax.all_gather(part, 'dev', axis=0, tiled=True)]
    all_gather x2, waiting for transfers between devices: 0.02 us -> 41.7 us  [all_sum(): outs.append(lax.all_gather(part, 'grp', axis=0, tiled=True))]
    all_to_all x4 -> x3, blocking collectives: 83.1 us -> 75.1 us  [the longest x1 45.9 us: all_sum(): both = lax.all_to_all(both, 'grp', 0, 0, tiled=False).sum(0)]
  transfers between devices with their start and end apart: 2 -> 2, of which waited for: 0 -> 1; matrix products, arithmetic and copies ran while one was open for 7% -> 7% of each run, Pallas kernels for 18% -> 19%
where the time goes in v5:
time: 308 us; the launch traced here: 305 us
  Pallas kernels  115 us (37%)
  blocking collectives  75.1 us (24%)
  matrix products  46.8 us (15%)
  waiting for transfers between devices  41.7 us (14%)
  between operations  14.4 us (5%)
  other arithmetic  6.23 us (2%)
  local copies, waits for them, and re-layouts  5.65 us (2%)
    pallas_call x8, Pallas kernels, base_inv(): pl.pallas_call(_base_kernel, out_shape=jax.ShapeDtypeStruct((n, n), jnp.f...  115 us
    all_to_all x1, blocking collectives, all_sum(): both = lax.all_to_all(both, 'grp', 0, 0, tiled=False).sum(0)  45.9 us
    all_gather x2, waiting for transfers between devices, all_sum(): outs.append(lax.all_gather(part, 'grp', axis=0, tiled=True))  41.7 us
    dot_general x14, matrix products, mm(): return jnp.dot(a, b, precision=HI)  18.6 us
    all_to_all x1, blocking collectives, all_sum(): both = lax.all_to_all(both, 'dev', 0, 0, tiled=False).sum(0)  17.8 us
    dot_general x14, matrix products, mmt(): return lax.dot_general(a, b, (((1,), (1,)), ((), ())), precision=HI)  17.7 us
    all_to_all x1, blocking collectives, all_sum(): both = lax.all_to_all(both, 'dev', 0, 0, tiled=False)  11.5 us
  transfers between devices with their start and end apart: 2, of which 1 were waited for; matrix products, arithmetic and copies ran while one was open for 7% of the time, Pallas kernels for 19%

profile of v5, /device:TPU:2, one launch (start us, length us, event | category | flops | bytes accessed | tf_op | source)
XLA Modules:
  0.0 304.9 jit_solution(7483445466089611073)
XLA Ops:
  7.2 0.7 select_convert_fusion
  7.9 4.5 %fusion.12 = bf16[512,1024]{1,0:T(8,128)(2,1)S(1)} fusion(bf16[2048,1024]{1,0:T(8,128)(2,1)} %param.4, s32[2048]{0:T(1024)} %param.6, bf16[2048]{0:T(1024)(128)(2,1)S(1)} %select_convert_fusion), kind=kOutput, calls=%fused_computation.14 | convolution fusion | flops 2150105088 | bytes 5255168 | tf_op jit(solution)/shard_map/dot_general | solution.py:115
  12.9 0.7 fusion.23
  14.1 45.9 %all_to_all.15 = f32[32,48,512]{2,1,0:T(8,128)S(1)} all-to-all(f32[32,48,512]{2,1,0:T(8,128)S(1)} %pad_maximum_fusion), channel_id=1, replica_groups=mesh['grp'=32,'dev'=8] {'grp'}, dimensions={0} | all-to-all | bytes 6291456 | tf_op jit(solution)/shard_map/all_to_all | solution.py:90
  60.4 17.8 %all_to_all.16 = f32[8,6,512]{2,1,0:T(8,128)S(1)} all-to-all(f32[8,6,512]{2,1,0:T(8,128)S(1)} %pad_maximum_fusion.1), channel_id=1, replica_groups=mesh['grp'=32,'dev'=8] {'dev'}, dimensions={0} | all-to-all | bytes 196608 | tf_op jit(solution)/shard_map/all_to_all | solution.py:95
  78.2 11.5 %all_to_all.17 = f32[8,6,512]{2,1,0:T(8,128)S(1)} all-to-all(f32[8,6,512]{2,1,0:T(8,128)S(1)} %broadcast_in_dim.10), channel_id=1, replica_groups=mesh['grp'=32,'dev'=8] {'dev'}, dimensions={0} | all-to-all | bytes 196608 | tf_op jit(solution)/shard_map/all_to_all | solution.py:97
  89.7 0.7 reshape.29
  91.3 41.7 %all-gather.3.cloned.1.call-done = f32[1024,512]{1,0:T(8,128)} async-done(((f32[32,512]{1,0:T(8,128)}), f32[1024,512]{1,0:T(8,128)}) %all-gather.3.cloned.1.call-update) | async-done | bytes 2097168 | tf_op jit(solution)/shard_map/all_gather | solution.py:101
  133.0 1.3 select_add_fusion.1
  134.9 14.3 %shard_map.46 = f32[128,128]{1,0:T(8,128)} custom-call(f32[128,128]{1,0:T(8,128)} %slice.110.a_ref), custom_call_target="tpu_custom_call" | custom-call | tf_op jit(solution)/shard_map/pallas_call | solution.py:61
  149.3 1.2 fusion.46
  150.4 1.0 fusion.61
  151.5 0.9 convolution_subtract_fusion.6.a_ref
  152.4 14.3 %shard_map.47 = f32[128,128]{1,0:T(8,128)} custom-call(f32[128,128]{1,0:T(8,128)} %convolution_subtract_fusion.6.a_ref), custom_call_target="tpu_custom_call" | custom-call | tf_op jit(solution)/shard_map/pallas_call | solution.py:61
  166.7 1.1 convolution_negate_fusion.6
  167.8 1.3 fusion.28
  170.2 14.3 %shard_map.48 = f32[128,128]{1,0:T(8,128)} custom-call(f32[128,128]{1,0:T(8,128)} %slice.115.a_ref), custom_call_target="tpu_custom_call" | custom-call | tf_op jit(solution)/shard_map/pallas_call | solution.py:61
  184.5 0.8 concatenate.86
  185.4 1.1 fusion.44
  186.5 0.9 convolution_subtract_fusion.5.a_ref
  187.4 14.3 %shard_map.49 = f32[128,128]{1,0:T(8,128)} custom-call(f32[128,128]{1,0:T(8,128)} %convolution_subtract_fusion.5.a_ref), custom_call_target="tpu_custom_call" | custom-call | tf_op jit(solution)/shard_map/pallas_call | solution.py:61
  201.7 0.9 select_maximum_fusion.4
  202.6 1.0 fusion.62
  203.7 1.0 convolution_negate_fusion.5
  205.1 1.2 convolution_negate_fusion.2
  206.3 3.1 %fusion.16 = f32[512,512]{1,0:T(8,128)S(1)} fusion(f32[1024,512]{1,0:T(8,128)} %all-gather.3.cloned.1.call-done, f32[256,256]{1,0:T(8,128)S(1)} %select_maximum_fusion.4, f32[128,128]{1,0:T(8,128)} %shard_map.49, f32[128,128]{1,0:T(8,128)S(1)} %convolution_negate_fusion.5, f32[128,256]{1,0:T(8,128)S(1)} %concatenate.86, ...), kind=kOutput, calls=%fused_computation.33 | convolution fusion | flops 1612185600 | bytes 2883584 | tf_op jit(solution)/shard_map/dot_general | solution.py:26
  209.4 2.8 fusion.57
  212.2 3.1 %convolution_subtract_fusion = f32[512,512]{1,0:T(8,128)S(1)} fusion(f32[512,512]{1,0:T(8,128)S(1)} %fusion.16, f32[512,512]{1,0:T(8,128)} %all-gather.5.cloned.1.call-done), kind=kOutput, calls=%fused_computation.18 | convolution fusion | flops 1611661312 | bytes 3145728 | tf_op jit(solution)/shard_map/dot_general | solution.py:26
  215.9 14.3 %shard_map.50 = f32[128,128]{1,0:T(8,128)} custom-call(f32[128,128]{1,0:T(8,128)} %slice.120.a_ref), custom_call_target="tpu_custom_call" | custom-call | tf_op jit(solution)/shard_map/pallas_call | solution.py:61
  230.3 1.2 fusion.42
  231.4 1.0 fusion.63
  232.5 0.9 convolution_subtract_fusion.4.a_ref
  233.4 14.5 %shard_map.51 = f32[128,128]{1,0:T(8,128)} custom-call(f32[128,128]{1,0:T(8,128)} %convolution_subtract_fusion.4.a_ref), custom_call_target="tpu_custom_call" | custom-call | tf_op jit(solution)/shard_map/pallas_call | solution.py:61
  247.8 1.0 convolution_negate_fusion.4
  248.9 1.3 fusion.26
  250.6 1.2 fusion.60
  251.9 0.9 select_maximum_fusion.3
  253.3 14.3 %shard_map.52 = f32[128,128]{1,0:T(8,128)} custom-call(f32[128,128]{1,0:T(8,128)} %slice.125.a_ref), custom_call_target="tpu_custom_call" | custom-call | tf_op jit(solution)/shard_map/pallas_call | solution.py:61
  267.7 1.1 fusion.40
  268.8 0.9 convolution_subtract_fusion.3.a_ref
  269.7 1.0 fusion.64
  270.7 0.9 concatenate.96
  271.6 14.3 %shard_map.53 = f32[128,128]{1,0:T(8,128)} custom-call(f32[128,128]{1,0:T(8,128)} %convolution_subtract_fusion.3.a_ref), custom_call_target="tpu_custom_call" | custom-call | tf_op jit(solution)/shard_map/pallas_call | solution.py:61
  285.9 1.1 convolution_negate_fusion.3
  287.0 1.2 convolution_negate_fusion.1
  288.3 1.1 fusion.25
  289.4 3.2 %fusion.15 = bf16[512,512]{1,0:T(8,128)(2,1)S(1)} fusion(f32[512,512]{1,0:T(8,128)} %fusion.57, f32[256,256]{1,0:T(8,128)S(1)} %select_maximum_fusion.3, f32[128,128]{1,0:T(8,128)S(1)} %copy-done.4, f32[128,128]{1,0:T(8,128)S(1)} %convolution_negate_fusion.3, f32[128,256]{1,0:T(8,128)S(1)} %concatenate.96, f32[256,256]{1,0:T(8,128)S(1)} %convolution_negate_fusion.1), kind=kOutput, calls=%fused_computation.19 | convolution fusion | flops 1612709888 | bytes 2359296 | tf_op jit(solution)/shard_map/dot_general | solution.py:22
  292.6 4.8 %multiply_reduce_fusion = f32[2048]{0:T(1024)S(1)} fusion(bf16[2048,1024]{1,0:T(8,128)(2,1)S(1)} %copy-done.5, bf16[512,512]{1,0:T(8,128)(2,1)S(1)} %get-tuple-element.6, bf16[512,512]{1,0:T(8,128)(2,1)S(1)} %get-tuple-element.5, bf16[512,512]{1,0:T(8,128)(2,1)S(1)} %fusion.15), kind=kOutput, calls=%fused_computation | convolution fusion | flops 4307548160 | bytes 5775360 | tf_op jit(solution)/shard_map/dot_general | solution.py:132
  (38 shorter events, 6.6 us)
Async XLA Ops:
  6.5 126.4 %all-gather.3.cloned.1.call-start = ((), (), s32[]{:S(2)}) async-start(), calls=%async_computation.3 | async-start | bytes 2162688 | tf_op jit(solution)/shard_map/all_gather | solution.py:101
  90.3 121.9 %all-gather.5.cloned.1.call-start = ((), (), s32[]{:S(2)}) async-start(), calls=%async_computation.4 | async-start | bytes 1081344 | tf_op jit(solution)/shard_map/all_gather | solution.py:101
  149.3 52.4 %copy-start = (f32[128,128]{1,0:T(8,128)S(1)}, f32[128,128]{1,0:T(8,128)}, u32[]{:S(2)}) copy-start(f32[128,128]{1,0:T(8,128)} %shard_map.46) | copy-start | bytes 196612
  166.7 38.0 %copy-start.2 = (f32[128,128]{1,0:T(8,128)S(1)}, f32[128,128]{1,0:T(8,128)}, u32[]{:S(2)}) copy-start(f32[128,128]{1,0:T(8,128)} %shard_map.47) | copy-start | bytes 196612
  201.7 7.7 %copy-start.3 = (f32[128,128]{1,0:T(8,128)S(1)}, f32[128,128]{1,0:T(8,128)}, u32[]{:S(2)}) copy-start(f32[128,128]{1,0:T(8,128)} %shard_map.49) | copy-start | bytes 196612
  230.2 21.6 %copy-start.1 = (f32[128,128]{1,0:T(8,128)S(1)}, f32[128,128]{1,0:T(8,128)}, u32[]{:S(2)}) copy-start(f32[128,128]{1,0:T(8,128)} %shard_map.50) | copy-start | bytes 196612
  285.9 3.5 %copy-start.4 = (f32[128,128]{1,0:T(8,128)S(1)}, f32[128,128]{1,0:T(8,128)}, u32[]{:S(2)}) copy-start(f32[128,128]{1,0:T(8,128)} %shard_map.53) | copy-start | bytes 196612
  288.3 4.4 %copy-start.5 = (bf16[2048,1024]{1,0:T(8,128)(2,1)S(1)}, bf16[2048,1024]{1,0:T(8,128)(2,1)}, u32[]{:S(2)}) copy-start(bf16[2048,1024]{1,0:T(8,128)(2,1)} %param.4) | copy-start | bytes 12582916
Sparse Core Ops, SparseCore 0:
  90.5 42.4 all-gather.2
  135.5 47.4 all-gather.4

commit v6 on v4

--- a/solution.py
+++ b/solution.py
@@ -112,11 +112,14 @@
     l21 = mmt(gram_left[h:], i11)
     i22 = chol_inv(gram_corner + ridge - mmt(l21, l21))
     i21 = -mm(i22, mm(l21, i11))
-    inverse = jnp.block([[i11, jnp.zeros((h, h), jnp.float32)], [i21, i22]])
-    weight = inverse.T.astype(jnp.bfloat16)
+    w11, w12, w22 = (x.T.astype(jnp.bfloat16) for x in (i11, i21, i22))
     factor = ridge_value / features
-    projected = jnp.dot(rows, weight, preferred_element_type=jnp.float32)
-    return jnp.where(is_live, factor * jnp.sum(projected * projected, axis=1), 0.0)
+    left = jnp.dot(rows[:, :h], w11, preferred_element_type=jnp.float32)
+    right = jnp.dot(rows[:, :h], w12, preferred_element_type=jnp.float32) + jnp.dot(
+        rows[:, h:], w22, preferred_element_type=jnp.float32
+    )
+    total = jnp.sum(left * left, axis=1) + jnp.sum(right * right, axis=1)
+    return jnp.where(is_live, factor * total, 0.0)
 
 
 def solution(mesh):

time: 294 us -> 295 us (level)
  no operation moved by 1% of the time
where the time goes in v6:
time: 295 us; the launch traced here: 292 us
  Pallas kernels  115 us (39%)
  blocking collectives  104 us (35%)
  matrix products  47.1 us (16%)
  between operations  14.4 us (5%)
  local copies, waits for them, and re-layouts  5.55 us (2%)
  other arithmetic  4.71 us (2%)
    pallas_call x8, Pallas kernels, base_inv(): pl.pallas_call(_base_kernel, out_shape=jax.ShapeDtypeStruct((n, n), jnp.f...  115 us
    all_to_all x2, blocking collectives, all_sum(): lax.all_to_all(g.reshape(n_grp, rows // n_grp, cols), 'grp', 0, 0, tiled=...  56.2 us
    all_to_all x2, blocking collectives, all_sum(): lax.all_to_all(part.reshape(n_dev, piece, cols), 'dev', 0, 0, tiled=False)  27 us
    all_to_all x2, blocking collectives, all_sum(): lax.all_to_all(part, 'dev', 0, 0, tiled=False).reshape(n_dev * piece, cols)  21.1 us
    dot_general x14, matrix products, mm(): return jnp.dot(a, b, precision=HI)  19.8 us
    dot_general x14, matrix products, mmt(): return lax.dot_general(a, b, (((1,), (1,)), ((), ())), precision=HI)  17.6 us
  transfers between devices with their start and end apart: 2, of which 1 were waited for; matrix products, arithmetic and copies ran while one was open for 8% of the time, Pallas kernels for 20%

profile of v6, /device:TPU:2, one launch (start us, length us, event | category | flops | bytes accessed | tf_op | source)
XLA Modules:
  0.0 291.7 jit_solution(15721478271795331293)
XLA Ops:
  7.9 4.5 %fusion.8 = bf16[512,1024]{1,0:T(8,128)(2,1)S(1)} fusion(bf16[2048,1024]{1,0:T(8,128)(2,1)} %param.4, s32[2048]{0:T(1024)} %param.6, bf16[2048]{0:T(1024)(128)(2,1)S(1)} %select_convert_fusion), kind=kOutput, calls=%fused_computation.10 | convolution fusion | flops 2150105088 | bytes 5255168 | tf_op jit(solution)/shard_map/dot_general | solution.py:103
  13.2 34.6 %all_to_all.30 = f32[32,32,512]{2,1,0:T(8,128)S(1)} all-to-all(f32[32,32,512]{2,1,0:T(8,128)S(1)} %bitcast.48), channel_id=1, replica_groups=mesh['grp'=32,'dev'=8] {'grp'}, dimensions={0} | all-to-all | bytes 4194304 | tf_op jit(solution)/shard_map/all_to_all | solution.py:85
  48.0 16.6 %all_to_all.31 = f32[8,4,512]{2,1,0:T(4,128)S(1)} all-to-all(f32[8,4,512]{2,1,0:T(4,128)S(1)} %reshape.27), channel_id=1, replica_groups=mesh['grp'=32,'dev'=8] {'dev'}, dimensions={0} | all-to-all | bytes 131072 | tf_op jit(solution)/shard_map/all_to_all | solution.py:87
  64.7 10.7 %all_to_all.32 = f32[8,4,512]{2,1,0:T(4,128)S(1)} all-to-all(f32[8,4,512]{2,1,0:T(4,128)S(1)} %broadcast_in_dim.12), channel_id=1, replica_groups=mesh['grp'=32,'dev'=8] {'dev'}, dimensions={0} | all-to-all | bytes 131072 | tf_op jit(solution)/shard_map/all_to_all | solution.py:89
  76.6 21.6 %all_to_all.33 = f32[32,16,512]{2,1,0:T(8,128)S(1)} all-to-all(f32[32,16,512]{2,1,0:T(8,128)S(1)} %bitcast.49), channel_id=1, replica_groups=mesh['grp'=32,'dev'=8] {'grp'}, dimensions={0} | all-to-all | bytes 2097152 | tf_op jit(solution)/shard_map/all_to_all | solution.py:85
  98.3 10.4 %all_to_all.34 = f32[8,2,512]{2,1,0:T(2,128)S(1)} all-to-all(f32[8,2,512]{2,1,0:T(2,128)S(1)} %reshape.30), channel_id=1, replica_groups=mesh['grp'=32,'dev'=8] {'dev'}, dimensions={0} | all-to-all | bytes 65536 | tf_op jit(solution)/shard_map/all_to_all | solution.py:87
  108.7 10.4 %all_to_all.35 = f32[8,2,512]{2,1,0:T(2,128)S(1)} all-to-all(f32[8,2,512]{2,1,0:T(2,128)S(1)} %broadcast_in_dim.13), channel_id=1, replica_groups=mesh['grp'=32,'dev'=8] {'dev'}, dimensions={0} | all-to-all | bytes 65536 | tf_op jit(solution)/shard_map/all_to_all | solution.py:89
  120.6 1.3 select_add_fusion.1
  122.5 14.3 %shard_map.46 = f32[128,128]{1,0:T(8,128)} custom-call(f32[128,128]{1,0:T(8,128)} %slice.99.a_ref), custom_call_target="tpu_custom_call" | custom-call | tf_op jit(solution)/shard_map/pallas_call | solution.py:61
  136.8 1.2 fusion.42
  138.0 1.0 fusion.56
  139.1 0.9 convolution_subtract_fusion.6.a_ref
  140.0 14.3 %shard_map.47 = f32[128,128]{1,0:T(8,128)} custom-call(f32[128,128]{1,0:T(8,128)} %convolution_subtract_fusion.6.a_ref), custom_call_target="tpu_custom_call" | custom-call | tf_op jit(solution)/shard_map/pallas_call | solution.py:61
  154.3 1.0 convolution_negate_fusion.6
  155.3 1.3 fusion.24
  157.7 14.3 %shard_map.48 = f32[128,128]{1,0:T(8,128)} custom-call(f32[128,128]{1,0:T(8,128)} %slice.104.a_ref), custom_call_target="tpu_custom_call" | custom-call | tf_op jit(solution)/shard_map/pallas_call | solution.py:61
  172.0 1.1 fusion.40
  173.1 0.9 convolution_subtract_fusion.5.a_ref
  174.8 14.3 %shard_map.49 = f32[128,128]{1,0:T(8,128)} custom-call(f32[128,128]{1,0:T(8,128)} %convolution_subtract_fusion.5.a_ref), custom_call_target="tpu_custom_call" | custom-call | tf_op jit(solution)/shard_map/pallas_call | solution.py:61
  189.2 0.9 select_maximum_fusion.5
  190.1 1.0 fusion.57
  191.1 1.0 convolution_negate_fusion.5
  192.2 1.2 fusion.54
  193.4 1.4 convolution_negate_fusion.2
  194.8 3.1 %fusion.12 = f32[512,512]{1,0:T(8,128)S(1)} fusion(f32[1024,512]{1,0:T(8,128)} %all-gather.3.cloned.1.call-done, f32[256,256]{1,0:T(8,128)S(1)} %select_maximum_fusion.5, f32[128,128]{1,0:T(8,128)} %shard_map.49, f32[128,128]{1,0:T(8,128)S(1)} %convolution_negate_fusion.5, f32[128,256]{1,0:T(8,128)S(1)} %concatenate.64, ...), kind=kOutput, calls=%fused_computation.29 | convolution fusion | flops 1612185600 | bytes 2883584 | tf_op jit(solution)/shard_map/dot_general | solution.py:26
  197.9 1.8 fusion.53
  199.7 1.3 multiply_reduce_fusion.1
  201.1 3.1 %convolution_subtract_fusion = f32[512,512]{1,0:T(8,128)S(1)} fusion(f32[512,512]{1,0:T(8,128)S(1)} %fusion.12, f32[512,512]{1,0:T(8,128)} %all-gather.5.cloned.1.call-done), kind=kOutput, calls=%fused_computation.14 | convolution fusion | flops 1611661312 | bytes 3145728 | tf_op jit(solution)/shard_map/dot_general | solution.py:26
  204.8 14.5 %shard_map.50 = f32[128,128]{1,0:T(8,128)} custom-call(f32[128,128]{1,0:T(8,128)} %slice.109.a_ref), custom_call_target="tpu_custom_call" | custom-call | tf_op jit(solution)/shard_map/pallas_call | solution.py:61
  219.2 1.1 fusion.38
  220.3 1.0 fusion.58
  221.4 0.9 convolution_subtract_fusion.4.a_ref
  222.3 14.3 %shard_map.51 = f32[128,128]{1,0:T(8,128)} custom-call(f32[128,128]{1,0:T(8,128)} %convolution_subtract_fusion.4.a_ref), custom_call_target="tpu_custom_call" | custom-call | tf_op jit(solution)/shard_map/pallas_call | solution.py:61
  236.6 1.0 convolution_negate_fusion.4
  237.7 1.3 fusion.22
  239.4 1.2 fusion.55
  240.6 0.9 select_maximum_fusion.4
  242.1 14.3 %shard_map.52 = f32[128,128]{1,0:T(8,128)} custom-call(f32[128,128]{1,0:T(8,128)} %slice.114.a_ref), custom_call_target="tpu_custom_call" | custom-call | tf_op jit(solution)/shard_map/pallas_call | solution.py:61
  256.4 1.1 fusion.36
  257.6 0.9 convolution_subtract_fusion.3.a_ref
  258.4 1.0 fusion.59
  259.5 0.9 concatenate.73
  260.3 14.3 %shard_map.53 = f32[128,128]{1,0:T(8,128)} custom-call(f32[128,128]{1,0:T(8,128)} %convolution_subtract_fusion.3.a_ref), custom_call_target="tpu_custom_call" | custom-call | tf_op jit(solution)/shard_map/pallas_call | solution.py:61
  274.7 1.2 convolution_negate_fusion.3
  275.9 1.3 convolution_negate_fusion.1
  277.2 4.4 %fusion.11 = bf16[512,512]{1,0:T(8,128)(2,1)S(1)} fusion(f32[512,512]{1,0:T(8,128)S(1)} %fusion.53, f32[256,256]{1,0:T(8,128)S(1)} %select_maximum_fusion.4, f32[128,128]{1,0:T(8,128)} %shard_map.53, f32[128,128]{1,0:T(8,128)S(1)} %convolution_negate_fusion.3, f32[128,256]{1,0:T(8,128)S(1)} %concatenate.73, f32[256,256]{1,0:T(8,128)S(1)} %convolution_negate_fusion.1), kind=kOutput, calls=%fused_computation.15 | convolution fusion | flops 1612709888 | bytes 2359296 | tf_op jit(solution)/shard_map/dot_general | solution.py:22
  281.6 1.3 fusion.5
  282.9 1.3 multiply_reduce_fusion
  (37 shorter events, 9.2 us)
Async XLA Ops:
  6.5 114.0 %all-gather.3.cloned.1.call-start = ((), (), s32[]{:S(2)}) async-start(), calls=%async_computation.6 | async-start | bytes 2162688 | tf_op jit(solution)/shard_map/all_gather | solution.py:90
  76.1 125.0 %all-gather.5.cloned.1.call-start = ((), (), s32[]{:S(2)}) async-start(), calls=%async_computation.7 | async-start | bytes 1081344 | tf_op jit(solution)/shard_map/all_gather | solution.py:90
  136.8 55.3 %copy-start = (f32[128,128]{1,0:T(8,128)S(1)}, f32[128,128]{1,0:T(8,128)}, u32[]{:S(2)}) copy-start(f32[128,128]{1,0:T(8,128)} %shard_map.46) | copy-start | bytes 196612
  189.2 8.7 %copy-start.3 = (f32[128,128]{1,0:T(8,128)S(1)}, f32[128,128]{1,0:T(8,128)}, u32[]{:S(2)}) copy-start(f32[128,128]{1,0:T(8,128)} %shard_map.49) | copy-start | bytes 196612
  193.4 6.3 %copy-start.1 = (bf16[2048,1024]{1,0:T(8,128)(2,1)S(1)}, bf16[2048,1024]{1,0:T(8,128)(2,1)}, u32[]{:S(2)}) copy-start(bf16[2048,1024]{1,0:T(8,128)(2,1)} %param.4) | copy-start | bytes 12582916
  274.7 6.9 %copy-start.2 = (bf16[2048,1024]{1,0:T(8,128)(2,1)S(1)}, bf16[2048,1024]{1,0:T(8,128)(2,1)}, u32[]{:S(2)}) copy-start(bf16[2048,1024]{1,0:T(8,128)(2,1)} %param.4) | copy-start | bytes 12582916
  281.6 1.3 copy-start.4
Sparse Core Ops, SparseCore 0:
  76.2 44.2 all-gather.2
  123.1 47.2 all-gather.4

commit v7 on v4

--- a/solution.py
+++ b/solution.py
@@ -57,10 +57,13 @@
 
 
 def base_inv(a):
-    n = a.shape[0]
+    n = BASE
     return pl.pallas_call(
         _base_kernel,
         out_shape=jax.ShapeDtypeStruct((n, n), jnp.float32),
+        grid=(1,),
+        in_specs=[pl.BlockSpec((n, n), lambda i: (0, 0))],
+        out_specs=pl.BlockSpec((n, n), lambda i: (0, 0)),
         scratch_shapes=[pltpu.VMEM((n, 2 * n), jnp.float32)],
     )(a)
 
@@ -70,7 +73,7 @@
     if n <= BASE:
         return base_inv(a)
     h = n // 2
-    i11 = chol_inv(a[:h, :h])
+    i11 = base_inv(a) if h <= BASE else chol_inv(a[:h, :h])
     l21 = mmt(a[h:, :h], i11)
     i22 = chol_inv(a[h:, h:] - mmt(l21, l21))
     i21 = -mm(i22, mm(l21, i11))

time: 294 us -> 296 us (level)
  matrix products: 46.9 us -> 50.1 us
    dot_general x14, matrix products: 17.7 us -> 20.9 us  [mmt(): return lax.dot_general(a, b, (((1,), (1,)), ((), ())), precision=HI)]
where the time goes in v7:
time: 296 us; the launch traced here: 293 us
  Pallas kernels  115 us (39%)
  blocking collectives  104 us (35%)
  matrix products  50.1 us (17%)
  between operations  14.3 us (5%)
  local copies, waits for them, and re-layouts  4.54 us (2%)
  other arithmetic  4.02 us (1%)
    pallas_call x8, Pallas kernels, base_inv(): pl.pallas_call(_base_kernel, out_shape=jax.ShapeDtypeStruct((n, n), jnp.f...  115 us
    all_to_all x2, blocking collectives, all_sum(): lax.all_to_all(g.reshape(n_grp, rows // n_grp, cols), 'grp', 0, 0, tiled=...  56.2 us
    all_to_all x2, blocking collectives, all_sum(): lax.all_to_all(part.reshape(n_dev, piece, cols), 'dev', 0, 0, tiled=False)  27 us
    all_to_all x2, blocking collectives, all_sum(): lax.all_to_all(part, 'dev', 0, 0, tiled=False).reshape(n_dev * piece, cols)  21.1 us
    dot_general x14, matrix products, mmt(): return lax.dot_general(a, b, (((1,), (1,)), ((), ())), precision=HI)  20.9 us
    dot_general x14, matrix products, mm(): return jnp.dot(a, b, precision=HI)  18.7 us
  transfers between devices with their start and end apart: 2, of which 1 were waited for; matrix products, arithmetic and copies ran while one was open for 8% of the time, Pallas kernels for 20%

profile of v7, /device:TPU:2, one launch (start us, length us, event | category | flops | bytes accessed | tf_op | source)
XLA Modules:
  0.0 292.9 jit_solution(17660210323493466601)
XLA Ops:
  7.9 4.5 %fusion.12 = bf16[512,1024]{1,0:T(8,128)(2,1)S(1)} fusion(bf16[2048,1024]{1,0:T(8,128)(2,1)} %param.4, s32[2048]{0:T(1024)} %param.6, bf16[2048]{0:T(1024)(128)(2,1)S(1)} %select_convert_fusion), kind=kOutput, calls=%fused_computation.13 | convolution fusion | flops 2150105088 | bytes 5255168 | tf_op jit(solution)/shard_map/dot_general | solution.py:106
  13.2 34.6 %all_to_all.30 = f32[32,32,512]{2,1,0:T(8,128)S(1)} all-to-all(f32[32,32,512]{2,1,0:T(8,128)S(1)} %bitcast.48), channel_id=1, replica_groups=mesh['grp'=32,'dev'=8] {'grp'}, dimensions={0} | all-to-all | bytes 4194304 | tf_op jit(solution)/shard_map/all_to_all | solution.py:88
  48.0 16.6 %all_to_all.31 = f32[8,4,512]{2,1,0:T(4,128)S(1)} all-to-all(f32[8,4,512]{2,1,0:T(4,128)S(1)} %reshape.27), channel_id=1, replica_groups=mesh['grp'=32,'dev'=8] {'dev'}, dimensions={0} | all-to-all | bytes 131072 | tf_op jit(solution)/shard_map/all_to_all | solution.py:90
  64.7 10.7 %all_to_all.32 = f32[8,4,512]{2,1,0:T(4,128)S(1)} all-to-all(f32[8,4,512]{2,1,0:T(4,128)S(1)} %broadcast_in_dim.12), channel_id=1, replica_groups=mesh['grp'=32,'dev'=8] {'dev'}, dimensions={0} | all-to-all | bytes 131072 | tf_op jit(solution)/shard_map/all_to_all | solution.py:92
  76.6 21.6 %all_to_all.33 = f32[32,16,512]{2,1,0:T(8,128)S(1)} all-to-all(f32[32,16,512]{2,1,0:T(8,128)S(1)} %bitcast.49), channel_id=1, replica_groups=mesh['grp'=32,'dev'=8] {'grp'}, dimensions={0} | all-to-all | bytes 2097152 | tf_op jit(solution)/shard_map/all_to_all | solution.py:88
  98.3 10.4 %all_to_all.34 = f32[8,2,512]{2,1,0:T(2,128)S(1)} all-to-all(f32[8,2,512]{2,1,0:T(2,128)S(1)} %reshape.30), channel_id=1, replica_groups=mesh['grp'=32,'dev'=8] {'dev'}, dimensions={0} | all-to-all | bytes 65536 | tf_op jit(solution)/shard_map/all_to_all | solution.py:90
  108.7 10.4 %all_to_all.35 = f32[8,2,512]{2,1,0:T(2,128)S(1)} all-to-all(f32[8,2,512]{2,1,0:T(2,128)S(1)} %broadcast_in_dim.13), channel_id=1, replica_groups=mesh['grp'=32,'dev'=8] {'dev'}, dimensions={0} | all-to-all | bytes 65536 | tf_op jit(solution)/shard_map/all_to_all | solution.py:92
  119.8 0.8 all-gather.3.cloned.1.call-done
  120.6 1.3 select_add_fusion.1
  122.6 14.3 %shard_map.46 = f32[128,128]{1,0:T(8,128)} custom-call(f32[256,256]{1,0:T(8,128)} %slice.78.a_ref), custom_call_target="tpu_custom_call" | custom-call | tf_op jit(solution)/shard_map/pallas_call | solution.py:61
  137.0 1.2 fusion.46
  138.1 1.0 fusion.61
  139.2 0.9 convolution_subtract_fusion.6.a_ref
  140.1 14.3 %shard_map.47 = f32[128,128]{1,0:T(8,128)} custom-call(f32[128,128]{1,0:T(8,128)} %convolution_subtract_fusion.6.a_ref), custom_call_target="tpu_custom_call" | custom-call | tf_op jit(solution)/shard_map/pallas_call | solution.py:61
  154.4 1.1 convolution_negate_fusion.6
  155.5 1.3 fusion.28
  156.8 1.1 convolution_subtract_fusion.2.a_ref
  157.9 14.3 %shard_map.48 = f32[128,128]{1,0:T(8,128)} custom-call(f32[256,256]{1,0:T(8,128)} %convolution_subtract_fusion.2.a_ref), custom_call_target="tpu_custom_call" | custom-call | tf_op jit(solution)/shard_map/pallas_call | solution.py:61
  172.3 1.1 fusion.44
  173.4 0.9 concatenate.78
  174.3 1.7 convolution_subtract_fusion.5.a_ref
  176.0 14.3 %shard_map.49 = f32[128,128]{1,0:T(8,128)} custom-call(f32[128,128]{1,0:T(8,128)} %convolution_subtract_fusion.5.a_ref), custom_call_target="tpu_custom_call" | custom-call | tf_op jit(solution)/shard_map/pallas_call | solution.py:61
  190.3 1.1 fusion.62
  191.4 1.0 convolution_negate_fusion.5
  192.8 1.2 convolution_negate_fusion.2
  194.1 3.1 %fusion.16 = f32[512,512]{1,0:T(8,128)S(1)} fusion(f32[1024,512]{1,0:T(8,128)} %all-gather.3.cloned.1.call-done, f32[256,256]{1,0:T(8,128)S(1)} %select_maximum_fusion.4, f32[128,128]{1,0:T(8,128)S(1)} %copy-done.4, f32[128,128]{1,0:T(8,128)S(1)} %convolution_negate_fusion.5, f32[128,256]{1,0:T(8,128)S(1)} %concatenate.78, ...), kind=kOutput, calls=%fused_computation.32 | convolution fusion | flops 1612185600 | bytes 2883584 | tf_op jit(solution)/shard_map/dot_general | solution.py:26
  197.2 2.8 fusion.57
  200.0 3.1 %convolution_subtract_fusion = f32[512,512]{1,0:T(8,128)S(1)} fusion(f32[512,512]{1,0:T(8,128)S(1)} %fusion.16, f32[512,512]{1,0:T(8,128)} %all-gather.5.cloned.1.call-done), kind=kOutput, calls=%fused_computation.17 | convolution fusion | flops 1611661312 | bytes 3145728 | tf_op jit(solution)/shard_map/dot_general | solution.py:26
  203.8 14.3 %shard_map.50 = f32[128,128]{1,0:T(8,128)} custom-call(f32[256,256]{1,0:T(8,128)} %slice.87.a_ref), custom_call_target="tpu_custom_call" | custom-call | tf_op jit(solution)/shard_map/pallas_call | solution.py:61
  218.2 1.2 fusion.42
  219.3 1.0 fusion.63
  220.4 0.9 convolution_subtract_fusion.4.a_ref
  221.3 14.4 %shard_map.51 = f32[128,128]{1,0:T(8,128)} custom-call(f32[128,128]{1,0:T(8,128)} %convolution_subtract_fusion.4.a_ref), custom_call_target="tpu_custom_call" | custom-call | tf_op jit(solution)/shard_map/pallas_call | solution.py:61
  235.7 1.1 convolution_negate_fusion.4
  236.9 1.3 fusion.26
  238.1 1.1 convolution_subtract_fusion.1.a_ref
  239.3 1.2 fusion.60
  240.5 14.3 %shard_map.52 = f32[128,128]{1,0:T(8,128)} custom-call(f32[256,256]{1,0:T(8,128)} %convolution_subtract_fusion.1.a_ref), custom_call_target="tpu_custom_call" | custom-call | tf_op jit(solution)/shard_map/pallas_call | solution.py:61
  254.8 1.1 fusion.40
  256.0 1.7 convolution_subtract_fusion.3.a_ref
  257.7 1.0 fusion.64
  258.7 0.9 concatenate.88
  259.6 14.3 %shard_map.53 = f32[128,128]{1,0:T(8,128)} custom-call(f32[128,128]{1,0:T(8,128)} %convolution_subtract_fusion.3.a_ref), custom_call_target="tpu_custom_call" | custom-call | tf_op jit(solution)/shard_map/pallas_call | solution.py:61
  273.9 1.1 convolution_negate_fusion.3
  275.1 1.2 convolution_negate_fusion.1
  276.3 1.0 fusion.25
  277.4 3.3 %fusion.15 = bf16[512,512]{1,0:T(8,128)(2,1)S(1)} fusion(f32[512,512]{1,0:T(8,128)} %fusion.57, f32[256,256]{1,0:T(8,128)S(1)} %select_maximum_fusion.3, f32[128,128]{1,0:T(8,128)S(1)} %copy-done.5, f32[128,128]{1,0:T(8,128)S(1)} %convolution_negate_fusion.3, f32[128,256]{1,0:T(8,128)S(1)} %concatenate.88, f32[256,256]{1,0:T(8,128)S(1)} %convolution_negate_fusion.1), kind=kOutput, calls=%fused_computation.18 | convolution fusion | flops 1612709888 | bytes 2359296 | tf_op jit(solution)/shard_map/dot_general | solution.py:22
  280.7 4.8 %multiply_reduce_fusion = f32[2048]{0:T(1024)S(1)} fusion(bf16[2048,1024]{1,0:T(8,128)(2,1)S(1)} %copy-done.6, bf16[512,512]{1,0:T(8,128)(2,1)S(1)} %fusion.58, bf16[512,512]{1,0:T(8,128)(2,1)S(1)} %fusion.25, bf16[512,512]{1,0:T(8,128)(2,1)S(1)} %fusion.15), kind=kOutput, calls=%fused_computation | convolution fusion | flops 4307548160 | bytes 5775360 | tf_op jit(solution)/shard_map/dot_general | solution.py:121
  (39 shorter events, 6.1 us)
Async XLA Ops:
  6.5 114.0 %all-gather.3.cloned.1.call-start = ((), (), s32[]{:S(2)}) async-start(), calls=%async_computation.6 | async-start | bytes 2162688 | tf_op jit(solution)/shard_map/all_gather | solution.py:93
  76.1 123.9 %all-gather.5.cloned.1.call-start = ((), (), s32[]{:S(2)}) async-start(), calls=%async_computation.7 | async-start | bytes 1081344 | tf_op jit(solution)/shard_map/all_gather | solution.py:93
  137.0 53.3 %copy-start = (f32[128,128]{1,0:T(8,128)S(1)}, f32[128,128]{1,0:T(8,128)}, u32[]{:S(2)}) copy-start(f32[128,128]{1,0:T(8,128)} %shard_map.46) | copy-start | bytes 196612
  154.4 35.9 %copy-start.2 = (f32[128,128]{1,0:T(8,128)S(1)}, f32[128,128]{1,0:T(8,128)}, u32[]{:S(2)}) copy-start(f32[128,128]{1,0:T(8,128)} %shard_map.47) | copy-start | bytes 196612
  190.3 3.8 %copy-start.4 = (f32[128,128]{1,0:T(8,128)S(1)}, f32[128,128]{1,0:T(8,128)}, u32[]{:S(2)}) copy-start(f32[128,128]{1,0:T(8,128)} %shard_map.49) | copy-start | bytes 196612
  218.2 21.1 %copy-start.1 = (f32[128,128]{1,0:T(8,128)S(1)}, f32[128,128]{1,0:T(8,128)}, u32[]{:S(2)}) copy-start(f32[128,128]{1,0:T(8,128)} %shard_map.50) | copy-start | bytes 196612
  235.7 23.9 %copy-start.3 = (f32[128,128]{1,0:T(8,128)S(1)}, f32[128,128]{1,0:T(8,128)}, u32[]{:S(2)}) copy-start(f32[128,128]{1,0:T(8,128)} %shard_map.51) | copy-start | bytes 196612
  273.9 3.4 %copy-start.5 = (f32[128,128]{1,0:T(8,128)S(1)}, f32[128,128]{1,0:T(8,128)}, u32[]{:S(2)}) copy-start(f32[128,128]{1,0:T(8,128)} %shard_map.53) | copy-start | bytes 196612
  276.3 4.4 %copy-start.6 = (bf16[2048,1024]{1,0:T(8,128)(2,1)S(1)}, bf16[2048,1024]{1,0:T(8,128)(2,1)}, u32[]{:S(2)}) copy-start(bf16[2048,1024]{1,0:T(8,128)(2,1)} %param.4) | copy-start | bytes 12582916
Sparse Core Ops, SparseCore 0:
  76.2 44.2 all-gather.2
  123.1 47.2 all-gather.4
